TPU v7x, 32 devices: a whole 2x2x4 slice. The times are simulated.
32 devices in a mesh: shard: 4 (over y, x), ctx: 4 (over z), tp: 2 (over core).
Axes of the slice: x: 2, y: 2, z: 4, core: 2. Of those that a mesh axis runs over, the one named last changes fastest.
Arguments:
- tokens: bfloat16 [10240, 768], P(('shard', 'ctx')), may hold values from -6 to 6
- seq_lengths: int32 [4], P('shard'), may hold values from 2240 to 2560
- query_weight: bfloat16 [768, 768], P('shard', 'tp'), may hold values from -0.21875 to 0.21875
- query_bias: bfloat16 [768], P(('shard', 'tp')), may hold values from -0.59765625 to 0.59765625
- key_weight: bfloat16 [768, 768], P('shard', 'tp'), may hold values from -0.21875 to 0.21875
- value_weight: bfloat16 [768, 768], P('shard', 'tp'), may hold values from -0.21875 to 0.21875
- value_bias: bfloat16 [768], P(('shard', 'tp')), may hold values from -0.119628906 to 0.119628906
- output_weight: bfloat16 [768, 768], P('shard', 'tp'), may hold values from -6 to 6
- output_bias: bfloat16 [768], P('shard'), may hold values from -0.59765625 to 0.59765625
- attn_gain: bfloat16 [768], P('shard'), may hold values from 0.5 to 1.5
- attn_shift: bfloat16 [768], P('shard'), may hold values from -0.59765625 to 0.59765625
- inner_weight: bfloat16 [768, 3072], P('shard', 'tp'), may hold values from -0.21875 to 0.21875
- inner_bias: bfloat16 [3072], P(('shard', 'tp')), may hold values from -0.59765625 to 0.59765625
- outer_weight: bfloat16 [768, 3072], P('shard', 'tp'), may hold values from -0.109375 to 0.109375
- outer_bias: bfloat16 [768], P('shard'), may hold values from -0.59765625 to 0.59765625
- final_gain: bfloat16 [768], P('shard'), may hold values from 0.5 to 1.5
- final_shift: bfloat16 [768], P('shard'), may hold values from -0.59765625 to 0.59765625
- upstream: bfloat16 [10240, 768], P(('shard', 'ctx')), may hold values from -6 to 6
Outputs:
- layer_out: bfloat16 [10240, 768], P(('shard', 'ctx'))
- tokens_gradient: float32 [10240, 768], P(('shard', 'ctx'))
- query_weight_gradient: float32 [768, 768], P('shard', 'tp')
- query_bias_gradient: float32 [768], P(('shard', 'tp'))
- key_weight_gradient: float32 [768, 768], P('shard', 'tp')
- value_weight_gradient: float32 [768, 768], P('shard', 'tp')
- value_bias_gradient: float32 [768], P(('shard', 'tp'))
- output_weight_gradient: float32 [768, 768], P('shard', 'tp')
- output_bias_gradient: float32 [768], P('shard')
- attn_gain_gradient: float32 [768], P('shard')
- attn_shift_gradient: float32 [768], P('shard')
- inner_weight_gradient: float32 [768, 3072], P('shard', 'tp')
- inner_bias_gradient: float32 [3072], P(('shard', 'tp'))
- outer_weight_gradient: float32 [768, 3072], P('shard', 'tp')
- outer_bias_gradient: float32 [768], P('shard')
- final_gain_gradient: float32 [768], P('shard')
- final_shift_gradient: float32 [768], P('shard')
All inputs are finite; a program needn't handle non-finite values.
Results may differ from a plain program's by a relative error of at most 0.014.
Values may be sent and summed in bfloat16 or wider, within the bound.
No kernel may reach another device: no remote copies, remote signals or barrier semaphores. Data moves between devices by JAX's collectives and lax.ppermute only.
A program may use at most 128 MiB of HBM per device.

v0:
```python
import jax
import jax.numpy as jnp
from jax import lax
from jax.sharding import PartitionSpec as P

HEAD_DIM = 64


EPSILON = 1e-12


def norm_parts(hidden):
    center = hidden - jnp.mean(hidden, -1, keepdims=True)
    inverse = lax.rsqrt(jnp.mean(center * center, -1, keepdims=True) + EPSILON)
    return (center * inverse, inverse)


def norm_back(gradient, normal_form, inverse, gain):
    scaled = gradient * gain
    inner = (
        scaled
        - jnp.mean(scaled, -1, keepdims=True)
        - normal_form * jnp.mean(scaled * normal_form, -1, keepdims=True)
    )
    return (inner * inverse, jnp.sum(gradient * normal_form, 0), jnp.sum(gradient, 0))


def exact_gelu(values):
    return jax.nn.gelu(values, approximate=False)


def on_device(
    tokens,
    seq_lengths,
    query_weight,
    query_bias,
    key_weight,
    value_weight,
    value_bias,
    output_weight,
    output_bias,
    attn_gain,
    attn_shift,
    inner_weight,
    inner_bias,
    outer_weight,
    outer_bias,
    final_gain,
    final_shift,
    upstream,
):
    row_count, model_width = tokens.shape
    tensor_place = lax.axis_index("tp")
    head_width = query_weight.shape[1]
    hidden_width = inner_weight.shape[1]
    head_count = head_width // HEAD_DIM
    factor = HEAD_DIM ** (-0.5)
    gathered = (
        lax.all_gather(query_weight, "shard", axis=0, tiled=True),
        lax.all_gather(key_weight, "shard", axis=0, tiled=True),
        lax.all_gather(value_weight, "shard", axis=0, tiled=True),
        lax.all_gather(output_weight, "shard", axis=0, tiled=True),
        lax.all_gather(inner_weight, "shard", axis=0, tiled=True),
        lax.all_gather(outer_weight, "shard", axis=0, tiled=True),
        lax.all_gather(output_bias, "shard", axis=0, tiled=True),
        lax.all_gather(attn_gain, "shard", axis=0, tiled=True),
        lax.all_gather(attn_shift, "shard", axis=0, tiled=True),
        lax.all_gather(outer_bias, "shard", axis=0, tiled=True),
        lax.all_gather(final_gain, "shard", axis=0, tiled=True),
        lax.all_gather(final_shift, "shard", axis=0, tiled=True),
    )
    (
        query_full,
        key_full,
        value_full,
        output_full,
        inner_full,
        outer_full,
        outbias_full,
        gain_first,
        shift_first,
        outerbias_full,
        gain_second,
        shift_second,
    ) = gathered
    vectors = (
        lax.all_gather(query_bias, ("shard", "tp"), axis=0, tiled=True),
        lax.all_gather(value_bias, ("shard", "tp"), axis=0, tiled=True),
        lax.all_gather(inner_bias, ("shard", "tp"), axis=0, tiled=True),
    )
    query_shift = lax.dynamic_slice_in_dim(
        vectors[0], tensor_place * head_width, head_width
    ).astype(jnp.float32)
    value_shift = lax.dynamic_slice_in_dim(
        vectors[1], tensor_place * head_width, head_width
    ).astype(jnp.float32)
    inner_shift = lax.dynamic_slice_in_dim(
        vectors[2], tensor_place * hidden_width, hidden_width
    ).astype(jnp.float32)
    query = (jnp.dot(tokens, query_full, preferred_element_type=jnp.float32) + query_shift).astype(
        jnp.bfloat16
    )
    key_local = jnp.dot(tokens, key_full, preferred_element_type=jnp.float32).astype(jnp.bfloat16)
    value_local = (
        jnp.dot(tokens, value_full, preferred_element_type=jnp.float32) + value_shift
    ).astype(jnp.bfloat16)
    keys, values = (
        lax.all_gather(key_local, "ctx", axis=0, tiled=True),
        lax.all_gather(value_local, "ctx", axis=0, tiled=True),
    )
    allowed = jnp.arange(keys.shape[0]) < seq_lengths[0]

    def split_heads(matrix):
        return matrix.reshape(matrix.shape[0], head_count, HEAD_DIM).transpose(1, 0, 2)

    def join_heads(stacked):
        return stacked.transpose(1, 0, 2).reshape(stacked.shape[1], head_width)

    def scores_of(query_head, key_head):
        scores = (
            jnp.einsum("qd,kd->qk", query_head, key_head, preferred_element_type=jnp.float32)
            * factor
        )
        return jnp.where(allowed[None, :], scores, -1e30)

    def head_forward(triple):
        query_head, key_head, value_head = triple
        scores = scores_of(query_head, key_head)
        highest = jnp.max(scores, -1, keepdims=True)
        shifted = jnp.exp(scores - highest)
        summed = jnp.sum(shifted, -1, keepdims=True)
        portion = (shifted / summed).astype(jnp.bfloat16)
        mixed = jnp.dot(portion, value_head, preferred_element_type=jnp.float32)
        return (mixed.astype(jnp.bfloat16), (highest + jnp.log(summed))[:, 0])

    query_heads = split_heads(query)
    key_heads = split_heads(keys)
    value_heads = split_heads(values)
    context_heads, log_sums = lax.map(head_forward, (query_heads, key_heads, value_heads))
    context = join_heads(context_heads)
    attn_part = jnp.einsum("th,oh->to", context, output_full, preferred_element_type=jnp.float32)
    attended = lax.psum(attn_part, "tp") + outbias_full.astype(jnp.float32)
    normal_first, inverse_first = norm_parts(tokens.astype(jnp.float32) + attended)
    normed = normal_first * gain_first.astype(jnp.float32) + shift_first.astype(jnp.float32)
    normed_low = normed.astype(jnp.bfloat16)
    hidden = jnp.dot(normed_low, inner_full, preferred_element_type=jnp.float32) + inner_shift
    active = exact_gelu(hidden).astype(jnp.bfloat16)
    branch_part = jnp.einsum("tf,of->to", active, outer_full, preferred_element_type=jnp.float32)
    branch = lax.psum(branch_part, "tp") + outerbias_full.astype(jnp.float32)
    normal_second, inverse_second = norm_parts(normed + branch)
    layer_out = (
        normal_second * gain_second.astype(jnp.float32) + shift_second.astype(jnp.float32)
    ).astype(jnp.bfloat16)
    regathered = (
        lax.all_gather(query_weight, "shard", axis=0, tiled=True),
        lax.all_gather(key_weight, "shard", axis=0, tiled=True),
        lax.all_gather(value_weight, "shard", axis=0, tiled=True),
        lax.all_gather(output_weight, "shard", axis=0, tiled=True),
        lax.all_gather(inner_weight, "shard", axis=0, tiled=True),
        lax.all_gather(outer_weight, "shard", axis=0, tiled=True),
        lax.all_gather(output_bias, "shard", axis=0, tiled=True),
        lax.all_gather(attn_gain, "shard", axis=0, tiled=True),
        lax.all_gather(attn_shift, "shard", axis=0, tiled=True),
        lax.all_gather(outer_bias, "shard", axis=0, tiled=True),
        lax.all_gather(final_gain, "shard", axis=0, tiled=True),
        lax.all_gather(final_shift, "shard", axis=0, tiled=True),
    )
    query_back, key_back, value_back, output_back, inner_back, outer_back = regathered[:6]
    gain_first_back = regathered[7].astype(jnp.float32)
    gain_second_back = regathered[10].astype(jnp.float32)
    dres_second, final_gain_part, final_shift_part = norm_back(
        upstream.astype(jnp.float32), normal_second, inverse_second, gain_second_back
    )
    dbranch = dres_second.astype(jnp.bfloat16)
    outer_bias_part = jnp.sum(dbranch.astype(jnp.float32), 0)
    outer_weight_part = jnp.einsum("to,tf->of", dbranch, active, preferred_element_type=jnp.float32)
    dactive = jnp.dot(dbranch, outer_back, preferred_element_type=jnp.float32)
    unused, gelu_pull = jax.vjp(exact_gelu, hidden)
    dhidden = gelu_pull(dactive)[0].astype(jnp.bfloat16)
    inner_weight_part = jnp.einsum(
        "td,tf->df", normed_low, dhidden, preferred_element_type=jnp.float32
    )
    inner_bias_part = jnp.sum(dhidden.astype(jnp.float32), 0)
    dnormed_part = jnp.einsum("tf,df->td", dhidden, inner_back, preferred_element_type=jnp.float32)
    dnormed = dres_second + lax.psum(dnormed_part, "tp")
    dres_first, attn_gain_part, attn_shift_part = norm_back(
        dnormed, normal_first, inverse_first, gain_first_back
    )
    dattended = dres_first.astype(jnp.bfloat16)
    output_bias_part = jnp.sum(dattended.astype(jnp.float32), 0)
    output_weight_part = jnp.einsum(
        "to,th->oh", dattended, context, preferred_element_type=jnp.float32
    )
    dcontext = jnp.dot(dattended, output_back, preferred_element_type=jnp.float32).astype(
        jnp.bfloat16
    )

    def head_backward(quintet):
        query_head, key_head, value_head, dcontext_head, log_sum = quintet
        portion = jnp.exp(scores_of(query_head, key_head) - log_sum[:, None])
        dportion = jnp.einsum(
            "qd,kd->qk", dcontext_head, value_head, preferred_element_type=jnp.float32
        )
        dvalue_head = jnp.einsum(
            "qk,qd->kd",
            portion.astype(jnp.bfloat16),
            dcontext_head,
            preferred_element_type=jnp.float32,
        )
        centering = jnp.sum(portion * dportion, -1, keepdims=True)
        dscores = (portion * (dportion - centering)).astype(jnp.bfloat16)
        dquery_head = jnp.dot(dscores, key_head, preferred_element_type=jnp.float32) * factor
        dkey_head = (
            jnp.einsum("qk,qd->kd", dscores, query_head, preferred_element_type=jnp.float32)
            * factor
        )
        return (dquery_head.astype(jnp.bfloat16), dkey_head, dvalue_head)

    dquery_heads, dkey_heads, dvalue_heads = lax.map(
        head_backward, (query_heads, key_heads, value_heads, split_heads(dcontext), log_sums)
    )
    dquery = join_heads(dquery_heads)
    dkeys_sum, dvalues_sum = (
        lax.psum_scatter(join_heads(dkey_heads), "ctx", scatter_dimension=0, tiled=True),
        lax.psum_scatter(join_heads(dvalue_heads), "ctx", scatter_dimension=0, tiled=True),
    )
    dkeys = dkeys_sum.astype(jnp.bfloat16)
    dvalues = dvalues_sum.astype(jnp.bfloat16)
    query_weight_part = jnp.einsum("td,th->dh", tokens, dquery, preferred_element_type=jnp.float32)
    key_weight_part = jnp.einsum("td,th->dh", tokens, dkeys, preferred_element_type=jnp.float32)
    value_weight_part = jnp.einsum("td,th->dh", tokens, dvalues, preferred_element_type=jnp.float32)
    query_bias_part = jnp.sum(dquery.astype(jnp.float32), 0)
    value_bias_part = jnp.sum(dvalues.astype(jnp.float32), 0)
    dinput_part = (
        jnp.einsum("th,dh->td", dquery, query_back, preferred_element_type=jnp.float32)
        + jnp.einsum("th,dh->td", dkeys, key_back, preferred_element_type=jnp.float32)
        + jnp.einsum("th,dh->td", dvalues, value_back, preferred_element_type=jnp.float32)
    )
    tokens_gradient = dres_first + lax.psum(dinput_part, "tp")
    (
        query_piece,
        key_piece,
        value_piece,
        output_piece,
        outbias_piece,
        inner_piece,
        outer_piece,
        outerbias_piece,
        final_gain_piece,
        final_shift_piece,
        attn_gain_piece,
        attn_shift_piece,
    ) = (
        lax.psum_scatter(query_weight_part, "shard", scatter_dimension=0, tiled=True),
        lax.psum_scatter(key_weight_part, "shard", scatter_dimension=0, tiled=True),
        lax.psum_scatter(value_weight_part, "shard", scatter_dimension=0, tiled=True),
        lax.psum_scatter(output_weight_part, "shard", scatter_dimension=0, tiled=True),
        lax.psum_scatter(output_bias_part, "shard", scatter_dimension=0, tiled=True),
        lax.psum_scatter(inner_weight_part, "shard", scatter_dimension=0, tiled=True),
        lax.psum_scatter(outer_weight_part, "shard", scatter_dimension=0, tiled=True),
        lax.psum_scatter(outer_bias_part, "shard", scatter_dimension=0, tiled=True),
        lax.psum_scatter(final_gain_part, "shard", scatter_dimension=0, tiled=True),
        lax.psum_scatter(final_shift_part, "shard", scatter_dimension=0, tiled=True),
        lax.psum_scatter(attn_gain_part, "shard", scatter_dimension=0, tiled=True),
        lax.psum_scatter(attn_shift_part, "shard", scatter_dimension=0, tiled=True),
    )
    query_bias_full = lax.dynamic_update_slice_in_dim(
        jnp.zeros((model_width,), jnp.float32), query_bias_part, tensor_place * head_width, 0
    )
    value_bias_full = lax.dynamic_update_slice_in_dim(
        jnp.zeros((model_width,), jnp.float32), value_bias_part, tensor_place * head_width, 0
    )
    inner_bias_full = lax.dynamic_update_slice_in_dim(
        jnp.zeros((hidden_width * lax.axis_size("tp"),), jnp.float32),
        inner_bias_part,
        tensor_place * hidden_width,
        0,
    )
    qbias_piece, vbias_piece, ibias_piece = (
        lax.psum_scatter(query_bias_full, ("shard", "tp"), scatter_dimension=0, tiled=True),
        lax.psum_scatter(value_bias_full, ("shard", "tp"), scatter_dimension=0, tiled=True),
        lax.psum_scatter(inner_bias_full, ("shard", "tp"), scatter_dimension=0, tiled=True),
    )
    (
        query_total,
        key_total,
        value_total,
        output_total,
        outbias_total,
        inner_total,
        outer_total,
        outerbias_total,
        final_gain_total,
        final_shift_total,
        attn_gain_total,
        attn_shift_total,
        qbias_total,
        vbias_total,
        ibias_total,
    ) = lax.psum(
        (
            query_piece,
            key_piece,
            value_piece,
            output_piece,
            outbias_piece,
            inner_piece,
            outer_piece,
            outerbias_piece,
            final_gain_piece,
            final_shift_piece,
            attn_gain_piece,
            attn_shift_piece,
            qbias_piece,
            vbias_piece,
            ibias_piece,
        ),
        "ctx",
    )
    return (
        layer_out,
        tokens_gradient,
        query_total,
        qbias_total,
        key_total,
        value_total,
        vbias_total,
        output_total,
        outbias_total,
        attn_gain_total,
        attn_shift_total,
        inner_total,
        ibias_total,
        outer_total,
        outerbias_total,
        final_gain_total,
        final_shift_total,
    )


def solution(mesh):
    placed = (
        P(("shard", "ctx"), None),
        P("shard"),
        P("shard", "tp"),
        P(("shard", "tp")),
        P("shard", "tp"),
        P("shard", "tp"),
        P(("shard", "tp")),
        P("shard", "tp"),
        P("shard"),
        P("shard"),
        P("shard"),
        P("shard", "tp"),
        P(("shard", "tp")),
        P("shard", "tp"),
        P("shard"),
        P("shard"),
        P("shard"),
        P(("shard", "ctx"), None),
    )
    return jax.shard_map(
        on_device,
        mesh=mesh,
        in_specs=placed,
        out_specs=(
            P(("shard", "ctx"), None),
            P(("shard", "ctx"), None),
            P("shard", "tp"),
            P(("shard", "tp")),
            P("shard", "tp"),
            P("shard", "tp"),
            P(("shard", "tp")),
            P("shard", "tp"),
            P("shard"),
            P("shard"),
            P("shard"),
            P("shard", "tp"),
            P(("shard", "tp")),
            P("shard", "tp"),
            P("shard"),
            P("shard"),
            P("shard"),
        ),
        check_vma=False,
    )
```

profile of v0, /device:TPU:0, one launch (start us, length us, event | category | flops | bytes accessed | tf_op | source)
XLA Modules:
  0.0 1034.5 jit_solution(1539145770249833474)
XLA Ops:
  8.1 12.4 %all_gather.63 = bf16[768,384]{1,0:T(8,128)(2,1)S(1)} all-gather(bf16[192,384]{1,0:T(8,128)(2,1)} %param.27), channel_id=1, replica_groups=mesh['shard'=4,'ctx'=4,'tp'=2] {'shard'}, dimensions={0}, use_global_device_ids=true | all-gather | bytes 737280 | tf_op jit(solution)/shard_map/all_gather | solution.py:61
  24.3 11.8 %all-reduce.21 = (bf16[768]{0:T(1024)(128)(2,1)S(1)}, bf16[768]{0:T(1024)(128)(2,1)S(1)}) all-reduce(bf16[768]{0:T(1024)(128)(2,1)S(1)} %dynamic-update-slice, bf16[768]{0:T(1024)(128)(2,1)S(1)} %dynamic-update-slice.1), channel_id=1, replica_groups=mesh['shard'=4,'ctx'=4,'tp'=2] {'shard','tp'}, use_global_device_ids=true, to_apply=%add | all-reduce | flops 1536 | bytes 6144
  39.0 9.8 all_gather.61
  51.1 10.6 %all_gather.59 = bf16[768,384]{1,0:T(8,128)(2,1)S(1)} all-gather(bf16[192,384]{1,0:T(8,128)(2,1)S(1)} %copy-done.21), channel_id=1, replica_groups=mesh['shard'=4,'ctx'=4,'tp'=2] {'shard'}, dimensions={0}, use_global_device_ids=true | all-gather | bytes 737280 | tf_op jit(solution)/shard_map/all_gather | solution.py:59
  64.6 9.9 all_gather.66
  88.1 38.8 %all-gather.6.cloned.1.call-done = bf16[2560,384]{1,0:T(8,128)(2,1)} async-done(((bf16[640,384]{1,0:T(8,128)(2,1)}), bf16[2560,384]{1,0:T(8,128)(2,1)}) %all-gather.6.cloned.1.call-update) | async-done | bytes 1966096 | tf_op jit(solution)/shard_map/all_gather | solution.py:108
  132.7 70.5 %while.28 = (s32[]{:T(128)}, bf16[6,640,64]{1,2,0:T(8,128)(2,1)S(1)}, f32[6,640]{1,0:T(8,128)}, bf16[6,640,64]{2,1,0:T(8,128)(2,1)}, bf16[6,2560,64]{2,1,0:T(8,1...) while((s32[]{:T(128)}, bf16[6,640,64]{1,2,0:T(8,128)(2,1)S(1)}, ...), condition=%wide.region_3.4_spmd.clone, body=%wide.region_0.3_spmd.clone.sunk | while | flops 439134080 | bytes 47478400 | solution.py:139
  208.6 17.2 %all-reduce.22 = (bf16[768]{0:T(1024)(128)(2,1)S(1)}, bf16[768]{0:T(1024)(128)(2,1)S(1)}, bf16[768]{0:T(1024)(128)(2,1)S(1)}, bf16[768]{0:T(1024)(128)(2,1)}, bf...) all-reduce(bf16[768]{0:T(1024)(128)(2,1)S(1)} %dynamic-update-slice, ...), channel_id=1, replica_groups=mesh['shard'=4,'ctx'=4,'tp'=2] {'shard'}, use_global_device_ids=true, to_apply=%add.2 | all-reduce | flops 4608 | bytes 18432
  243.8 13.1 %multiply_convert_fusion.1 = (bf16[640,1536]{1,0:T(8,128)(2,1)}, f32[640,1536]{1,0:T(8,128)}, f32[640,1536]{1,0:T(8,128)}) fusion(f32[1536]{0:T(1024)} %dynamic-slice_convert_fusion, bf16[768,1536]{1,0:T(8,128)(2,1)} %all-gather.10.cloned.1.call-done, f32[640,768]{1,0:T(8,128)S(1)} %get-tuple-element.323, f32[768]{0:T(1024)S(1)} %convert_element_type.110, ...), kind=kOutput, calls=%fused_computation.63 | convolution fusion | flops 1577287680 | bytes 14173184 | tf_op jit(solution)/shard_map/dot_general | solution.py:146
  257.0 25.8 %all-gather.12.cloned.1.call-done = bf16[768,1536]{1,0:T(8,128)(2,1)} async-done(((bf16[192,1536]{1,0:T(8,128)(2,1)}), bf16[768,1536]{1,0:T(8,128)(2,1)}) %all-gather.12.cloned.1.call-update) | async-done | bytes 2359312 | tf_op jit(solution)/shard_map/all_gather | solution.py:64
  290.7 18.6 %all-reduce.31.cloned.1.call-done = f32[640,768]{1,0:T(8,128)} async-done(((f32[640,768]{1,0:T(8,128)}), f32[640,768]{1,0:T(8,128)}) %all-reduce.31.cloned.1.call-update) | async-done | bytes 1966096 | tf_op jit(solution)/shard_map/psum | solution.py:149
  324.4 22.1 %all-reduce.33.cloned.1.call-done = f32[640,768]{1,0:T(8,128)} async-done(((f32[640,768]{1,0:T(8,128)}), f32[640,768]{1,0:T(8,128)}) %all-reduce.33.cloned.1.call-update) | async-done | bytes 1966096 | tf_op jit(solution)/shard_map/psum | solution.py:185
  355.5 92.1 %while.29 = (s32[]{:T(128)}, bf16[6,640,64]{1,2,0:T(8,128)(2,1)}, f32[6,2560,64]{1,2,0:T(8,128)}, f32[6,2560,64]{1,2,0:T(8,128)}, bf16[6,640,64]{2,1,0:T(8,128)(...) while((s32[]{:T(128)}, bf16[6,640,64]{1,2,0:T(8,128)(2,1)}, ...), condition=%wide.region_17.18_spmd.clone, body=%wide.region_15.17_spmd.clone.sunk | while | flops 1063569280 | bytes 53189236 | solution.py:219
  451.6 70.1 %reduce-scatter.15.cloned.1.call-done = f32[640,384]{0,1:T(8,128)} async-done(((f32[2560,384]{0,1:T(8,128)}), f32[640,384]{0,1:T(8,128)}) %reduce-scatter.15.cloned.1.call-update) | async-done | bytes 983056 | tf_op jit(solution)/shard_map/reduce_scatter | solution.py:224
  524.9 72.1 %reduce-scatter.17.cloned.1.call-done = f32[640,384]{0,1:T(8,128)} async-done(((f32[2560,384]{0,1:T(8,128)}), f32[640,384]{0,1:T(8,128)}) %reduce-scatter.17.cloned.1.call-update) | async-done | bytes 983056 | tf_op jit(solution)/shard_map/reduce_scatter | solution.py:225
  631.5 30.4 %reduce-scatter.27.cloned.1.call-done = f32[192,384]{1,0:T(8,128)} async-done(((f32[768,384]{1,0:T(8,128)}), f32[192,384]{1,0:T(8,128)}) %reduce-scatter.27.cloned.1.call-update) | async-done | bytes 294928
  663.8 29.6 %reduce-scatter.29.cloned.1.call-done = f32[192,384]{1,0:T(8,128)} async-done(((f32[768,384]{1,0:T(8,128)}), f32[192,384]{1,0:T(8,128)}) %reduce-scatter.29.cloned.1.call-update) | async-done | bytes 294928
  695.3 29.8 %reduce-scatter.19.cloned.1.call-done = f32[192,384]{1,0:T(8,128)} async-done(((f32[768,384]{1,0:T(8,128)}), f32[192,384]{1,0:T(8,128)}) %reduce-scatter.19.cloned.1.call-update) | async-done | bytes 294928 | tf_op jit(solution)/shard_map/reduce_scatter | solution.py:257
  725.1 59.9 %reduce-scatter.21.cloned.1.call-done = f32[192,1536]{1,0:T(8,128)} async-done(((f32[768,1536]{1,0:T(8,128)}), f32[192,1536]{1,0:T(8,128)}) %reduce-scatter.21.cloned.1.call-update) | async-done | bytes 1179664 | tf_op jit(solution)/shard_map/reduce_scatter | solution.py:259
  784.9 60.0 %reduce-scatter.23.cloned.1.call-done = f32[192,1536]{1,0:T(8,128)} async-done(((f32[768,1536]{1,0:T(8,128)}), f32[192,1536]{1,0:T(8,128)}) %reduce-scatter.23.cloned.1.call-update) | async-done | bytes 1179664 | tf_op jit(solution)/shard_map/reduce_scatter | solution.py:260
  847.2 15.3 %all-reduce.20 = (f32[768]{0:T(1024)S(1)}, f32[768]{0:T(1024)S(1)}, f32[768]{0:T(1024)S(1)}, f32[768]{0:T(1024)S(1)}, f32[768]{0:T(1024)S(1)}, /*index=5*/f32[768]{0:T(1024)S(1)}) all-reduce(f32[768]{0:T(1024)S(1)} %copy-done.30, f32[768]{0:T(1024)S(1)} %get-tuple-element.239, ...), channel_id=10, replica_groups=mesh['shard'=4,'ctx'=4,'tp'=2] {'shard'}, use_global_device_ids=true, to_apply=%region_36.37.clone | all-reduce | flops 4608 | bytes 36864
  864.9 22.8 %all-reduce.17 = (f32[768]{0:T(1024)S(1)}, f32[768]{0:T(1024)S(1)}, f32[3072]{0:T(1024)S(1)}) all-reduce(f32[768]{0:T(1024)S(1)} %dynamic_update_slice.27, f32[768]{0:T(1024)S(1)} %dynamic_update_slice.28, f32[3072]{0:T(1024)S(1)} %dynamic_update_slice.29), channel_id=5, replica_groups=mesh['shard'=4,'ctx'=4,'tp'=2] {'shard','tp'}, use_global_device_ids=true, to_apply=%region_24.25.clone | all-reduce | flops 4608 | bytes 36864
  887.9 14.1 %all-reduce.18 = (f32[96]{0:T(128)}, f32[96]{0:T(128)}, f32[192]{0:T(256)}, f32[192]{0:T(256)}, f32[192]{0:T(256)}, /*index=5*/f32[384]{0:T(512)}, f32[192]{0:T(256)}, f32[192]{0:T(256)}, f32[192]{0:T(256)}) all-reduce(f32[96]{0:T(128)S(1)} %dynamic-slice.9, ...), channel_id=1, replica_groups=mesh['shard'=4,'ctx'=4,'tp'=2] {'ctx'}, use_global_device_ids=true, to_apply=%region_25.26 | all-reduce | flops 1728 | bytes 13824 | tf_op jit(solution)/shard_map/psum | solution.py:300
  905.1 112.5 %all-reduce.37.cloned.1.call-done = (f32[192,384]{0,1:T(8,128)}, f32[192,384]{0,1:T(8,128)}, f32[192,384]{0,1:T(8,128)}, f32[192,384]{1,0:T(8,128)}, f32[192,1536]{1,0:T(8,128)}, /*index=5*/f32[192,1536]{1,0:T(8,128)}) async-done(((f32[192,384]{0,1:T(8,128)}, f32[192,384]{0,1:T(8,128)}, f32[192,384]{0,1:T(8,128)}, f32[192,384]{1,0:T(8,128)}, f32[192,1536]{1,0:T(8,128)}, /*index=5*/f32[192,1536]{1,0:T(8,128)}), ...) | async-done | bytes 3538960 | tf_op jit(solution)/shard_map/psum | solution.py:300
  (336 shorter events, 307.9 us)
Async XLA Ops:
  8.0 74.3 %all-gather.8.cloned.1.call-start = ((), (), s32[]{:S(2)}) async-start(), calls=%async_computation.9 | async-start | bytes 2457600 | tf_op jit(solution)/shard_map/all_gather | solution.py:109
  38.9 87.9 %all-gather.6.cloned.1.call-start = ((), (), s32[]{:S(2)}) async-start(), calls=%async_computation.8 | async-start | bytes 2457600 | tf_op jit(solution)/shard_map/all_gather | solution.py:108
  51.0 183.7 %all-reduce.29.cloned.1.call-start = ((), (), s32[]{:S(2)}) async-start(), calls=%async_computation.10 | async-start | bytes 3932160 | tf_op jit(solution)/shard_map/psum | solution.py:142
  205.3 38.5 %all-gather.10.cloned.1.call-start = ((), (), s32[]{:S(2)}) async-start(), calls=%async_computation.11 | async-start | bytes 2949120 | tf_op jit(solution)/shard_map/all_gather | solution.py:63
  205.9 76.9 %all-gather.12.cloned.1.call-start = ((), (), s32[]{:S(2)}) async-start(), calls=%async_computation.12 | async-start | bytes 2949120 | tf_op jit(solution)/shard_map/all_gather | solution.py:64
  206.5 102.8 %all-reduce.31.cloned.1.call-start = ((), (), s32[]{:S(2)}) async-start(), calls=%async_computation.13 | async-start | bytes 3932160 | tf_op jit(solution)/shard_map/psum | solution.py:149
  288.1 58.5 %all-reduce.33.cloned.1.call-start = ((), (), s32[]{:S(2)}) async-start(), calls=%async_computation.14 | async-start | bytes 3932160 | tf_op jit(solution)/shard_map/psum | solution.py:185
  324.1 197.5 %reduce-scatter.15.cloned.1.call-start = ((), (), s32[]{:S(2)}) async-start(), calls=%async_computation.15 | async-start | bytes 4915200 | tf_op jit(solution)/shard_map/reduce_scatter | solution.py:224
  447.6 149.4 %reduce-scatter.17.cloned.1.call-start = ((), (), s32[]{:S(2)}) async-start(), calls=%async_computation.16 | async-start | bytes 4915200 | tf_op jit(solution)/shard_map/reduce_scatter | solution.py:225
  448.4 181.3 %reduce-scatter.25.cloned.1.call-start = ((), (), s32[]{:S(2)}) async-start(), calls=%async_computation.21 | async-start | bytes 1474560
  451.5 210.4 %reduce-scatter.27.cloned.1.call-start = ((), (), s32[]{:S(2)}) async-start(), calls=%async_computation.22 | async-start | bytes 1474560
  524.9 168.5 %reduce-scatter.29.cloned.1.call-start = ((), (), s32[]{:S(2)}) async-start(), calls=%async_computation.23 | async-start | bytes 1474560
  600.3 124.8 %reduce-scatter.19.cloned.1.call-start = ((), (), s32[]{:S(2)}) async-start(), calls=%async_computation.18 | async-start | bytes 1474560 | tf_op jit(solution)/shard_map/reduce_scatter | solution.py:257
  603.9 181.0 %reduce-scatter.21.cloned.1.call-start = ((), (), s32[]{:S(2)}) async-start(), calls=%async_computation.19 | async-start | bytes 5898240 | tf_op jit(solution)/shard_map/reduce_scatter | solution.py:259
  610.2 234.7 %reduce-scatter.23.cloned.1.call-start = ((), (), s32[]{:S(2)}) async-start(), calls=%async_computation.20 | async-start | bytes 5898240 | tf_op jit(solution)/shard_map/reduce_scatter | solution.py:260
  617.6 284.4 %all-reduce.35.cloned.1.call-start = ((), (), s32[]{:S(2)}) async-start(), calls=%async_computation.17 | async-start | bytes 3932160 | tf_op jit(solution)/shard_map/psum | solution.py:239
  622.6 224.3 %copy-start.31 = (f32[1536]{0:T(1024)S(1)}, f32[1536]{0:T(1024)}, u32[]{:S(2)}) copy-start(f32[1536]{0:T(1024)} %get-tuple-element.334) | copy-start | bytes 18436
  622.6 224.6 %copy-start.24 = (f32[768]{0:T(1024)S(1)}, f32[768]{0:T(1024)}, u32[]{:S(2)}) copy-start(f32[768]{0:T(1024)} %get-tuple-element.241) | copy-start | bytes 9220
  622.6 224.6 %copy-start.25 = (f32[768]{0:T(1024)S(1)}, f32[768]{0:T(1024)}, u32[]{:S(2)}) copy-start(f32[768]{0:T(1024)} %get-tuple-element.246) | copy-start | bytes 9220
  622.6 224.6 %copy-start.26 = (f32[768]{0:T(1024)S(1)}, f32[768]{0:T(1024)}, u32[]{:S(2)}) copy-start(f32[768]{0:T(1024)} %get-tuple-element.313) | copy-start | bytes 9220
  622.6 224.6 %copy-start.27 = (f32[768]{0:T(1024)S(1)}, f32[768]{0:T(1024)}, u32[]{:S(2)}) copy-start(f32[768]{0:T(1024)} %get-tuple-element.244) | copy-start | bytes 9220
  622.6 224.6 %copy-start.30 = (f32[768]{0:T(1024)S(1)}, f32[768]{0:T(1024)}, u32[]{:S(2)}) copy-start(f32[768]{0:T(1024)} %get-tuple-element.315) | copy-start | bytes 9220
  622.6 394.9 %all-reduce.37.cloned.1.call-start = ((), (), s32[]{:S(2)}) async-start(), calls=%async_computation.24 | async-start | bytes 7667712 | tf_op jit(solution)/shard_map/psum | solution.py:300
  631.5 270.5 %copy-start.4 = (f32[640,768]{1,0:T(8,128)S(1)}, f32[640,768]{1,0:T(8,128)}, u32[]{:S(2)}) copy-start(f32[640,768]{1,0:T(8,128)} %copy-done.3) | copy-start | bytes 5898244
  (44 other events, 508.1 us)
Sparse Core Ops, SparseCore 0:
  39.0 43.2 all-gather.7
  84.5 42.3 all-gather.5
  205.5 19.8 all-reduce.28
  288.2 21.0 all-reduce.30
  324.3 22.2 all-reduce.32
  447.8 73.8 reduce-scatter.14
  523.9 73.0 reduce-scatter.16
  600.5 29.1 reduce-scatter.24
  633.1 28.6 reduce-scatter.26
  664.6 28.6 reduce-scatter.28
  696.3 28.6 reduce-scatter.18
  727.9 56.9 reduce-scatter.20
  787.9 56.9 reduce-scatter.22
  847.7 21.0 all-reduce.34
  872.0 145.4 all-reduce.36
Sparse Core Ops, SparseCore 1:
  207.7 36.1 all-gather.9
  245.6 37.2 all-gather.11
where the time goes:
time: 1050 us; the launch traced here: 1030 us
  waiting for transfers between devices  593 us (56%)
  matrix products  180 us (17%)
  blocking collectives  132 us (13%)
  local copies, waits for them, and re-layouts  66.1 us (6%)
  other arithmetic  42 us (4%)
  between operations  19.7 us (2%)
    psum x1, waiting for transfers between devices, on_device(): lax.psum((query_piece, key_piece, value_piece, output_piece, outbias_piec...  112 us
    reduce_scatter x1, waiting for transfers between devices, on_device(): lax.psum_scatter(join_heads(dvalue_heads), 'ctx', scatter_dimension=0, ti...  72.1 us
    reduce_scatter x1, waiting for transfers between devices, on_device(): lax.psum_scatter(join_heads(dkey_heads), 'ctx', scatter_dimension=0, tile...  70.1 us
    unnamed x20, waiting for transfers between devices  68.9 us
    unnamed x4, blocking collectives  67.1 us
    reduce_scatter x1, waiting for transfers between devices, on_device(): lax.psum_scatter(outer_weight_part, 'shard', scatter_dimension=0, tiled=T...  60 us
    reduce_scatter x1, waiting for transfers between devices, on_device(): lax.psum_scatter(inner_weight_part, 'shard', scatter_dimension=0, tiled=T...  59.9 us
    all_gather x1, waiting for transfers between devices, on_device(): lax.all_gather(key_local, 'ctx', axis=0, tiled=True)  38.8 us
  transfers between devices with their start and end apart: 17, of which 15 were waited for; matrix products, arithmetic and copies ran while one was open for 7% of the time, Pallas kernels for 0%

commit v1 on v0

v1 whole, which is shorter than its diff:
```python
import jax
import jax.numpy as jnp
from jax import lax
from jax.sharding import PartitionSpec as P

HEAD_DIM = 64


EPSILON = 1e-12


def norm_parts(hidden):
    center = hidden - jnp.mean(hidden, -1, keepdims=True)
    inverse = lax.rsqrt(jnp.mean(center * center, -1, keepdims=True) + EPSILON)
    return (center * inverse, inverse)


def norm_back(gradient, normal_form, inverse, gain):
    scaled = gradient * gain
    inner = (
        scaled
        - jnp.mean(scaled, -1, keepdims=True)
        - normal_form * jnp.mean(scaled * normal_form, -1, keepdims=True)
    )
    return (inner * inverse, jnp.sum(gradient * normal_form, 0), jnp.sum(gradient, 0))


def exact_gelu(values):
    return jax.nn.gelu(values, approximate=False)


def tp_sum(value):
    if lax.axis_size("tp") == 2:
        return value + lax.ppermute(value, "tp", [(0, 1), (1, 0)])
    return lax.psum(value, "tp")


def on_device(
    tokens,
    seq_lengths,
    query_weight,
    query_bias,
    key_weight,
    value_weight,
    value_bias,
    output_weight,
    output_bias,
    attn_gain,
    attn_shift,
    inner_weight,
    inner_bias,
    outer_weight,
    outer_bias,
    final_gain,
    final_shift,
    upstream,
):
    row_count, model_width = tokens.shape
    tensor_place = lax.axis_index("tp")
    tensor_count = lax.axis_size("tp")
    head_width = query_weight.shape[1]
    hidden_width = inner_weight.shape[1]
    head_count = head_width // HEAD_DIM
    factor = HEAD_DIM ** (-0.5)
    f32 = jnp.float32

    qkv_full = lax.all_gather(
        jnp.concatenate([query_weight, key_weight, value_weight], axis=1),
        "shard", axis=0, tiled=True,
    )
    query_full = qkv_full[:, :head_width]
    key_full = qkv_full[:, head_width : 2 * head_width]
    value_full = qkv_full[:, 2 * head_width :]
    rest_full = lax.all_gather(
        jnp.concatenate([output_weight, inner_weight, outer_weight], axis=1),
        "shard", axis=0, tiled=True,
    )
    output_full = rest_full[:, :head_width]
    inner_full = rest_full[:, head_width : head_width + hidden_width]
    outer_full = rest_full[:, head_width + hidden_width :]

    shard_vectors = (output_bias, attn_gain, attn_shift, outer_bias, final_gain, final_shift)
    piece = output_bias.shape[0]
    packed = jnp.concatenate(shard_vectors + (query_bias, value_bias, inner_bias))
    gathered = lax.all_gather(packed, ("shard", "tp"), axis=0)
    by_shard = gathered[::tensor_count, : 6 * piece].reshape(-1, 6, piece)
    full_vectors = by_shard.transpose(1, 0, 2).reshape(6, -1).astype(f32)
    outbias_full, gain_first, shift_first, outerbias_full, gain_second, shift_second = full_vectors
    offset = 6 * piece
    qb = query_bias.shape[0]
    ib = inner_bias.shape[0]
    qbias_all = gathered[:, offset : offset + qb].reshape(-1)
    vbias_all = gathered[:, offset + qb : offset + 2 * qb].reshape(-1)
    ibias_all = gathered[:, offset + 2 * qb : offset + 2 * qb + ib].reshape(-1)
    query_shift = lax.dynamic_slice_in_dim(qbias_all, tensor_place * head_width, head_width).astype(f32)
    value_shift = lax.dynamic_slice_in_dim(vbias_all, tensor_place * head_width, head_width).astype(f32)
    inner_shift = lax.dynamic_slice_in_dim(ibias_all, tensor_place * hidden_width, hidden_width).astype(f32)

    projected = jnp.dot(tokens, qkv_full, preferred_element_type=f32)
    query = (projected[:, :head_width] + query_shift).astype(jnp.bfloat16)
    key_local = projected[:, head_width : 2 * head_width].astype(jnp.bfloat16)
    value_local = (projected[:, 2 * head_width :] + value_shift).astype(jnp.bfloat16)
    kv = lax.all_gather(
        jnp.concatenate([key_local, value_local], axis=1), "ctx", axis=0, tiled=True
    )
    keys = kv[:, :head_width]
    values = kv[:, head_width:]
    allowed = jnp.arange(keys.shape[0]) < seq_lengths[0]

    def split_heads(matrix):
        return matrix.reshape(matrix.shape[0], head_count, HEAD_DIM).transpose(1, 0, 2)

    def join_heads(stacked):
        return stacked.transpose(1, 0, 2).reshape(stacked.shape[1], head_width)

    def scores_of(query_head, key_head):
        scores = (
            jnp.einsum("qd,kd->qk", query_head, key_head, preferred_element_type=f32)
            * factor
        )
        return jnp.where(allowed[None, :], scores, -1e30)

    def head_forward(triple):
        query_head, key_head, value_head = triple
        scores = scores_of(query_head, key_head)
        highest = jnp.max(scores, -1, keepdims=True)
        shifted = jnp.exp(scores - highest)
        summed = jnp.sum(shifted, -1, keepdims=True)
        portion = (shifted / summed).astype(jnp.bfloat16)
        mixed = jnp.dot(portion, value_head, preferred_element_type=f32)
        return (mixed.astype(jnp.bfloat16), (highest + jnp.log(summed))[:, 0])

    query_heads = split_heads(query)
    key_heads = split_heads(keys)
    value_heads = split_heads(values)
    context_heads, log_sums = lax.map(head_forward, (query_heads, key_heads, value_heads))
    context = join_heads(context_heads)
    attn_part = jnp.einsum("th,oh->to", context, output_full, preferred_element_type=f32)
    attended = tp_sum(attn_part) + outbias_full
    normal_first, inverse_first = norm_parts(tokens.astype(f32) + attended)
    normed = normal_first * gain_first + shift_first
    normed_low = normed.astype(jnp.bfloat16)
    hidden = jnp.dot(normed_low, inner_full, preferred_element_type=f32) + inner_shift
    active = exact_gelu(hidden).astype(jnp.bfloat16)
    branch_part = jnp.einsum("tf,of->to", active, outer_full, preferred_element_type=f32)
    branch = tp_sum(branch_part) + outerbias_full
    normal_second, inverse_second = norm_parts(normed + branch)
    layer_out = (normal_second * gain_second + shift_second).astype(jnp.bfloat16)

    dres_second, final_gain_part, final_shift_part = norm_back(
        upstream.astype(f32), normal_second, inverse_second, gain_second
    )
    dbranch = dres_second.astype(jnp.bfloat16)
    outer_bias_part = jnp.sum(dbranch.astype(f32), 0)
    outer_weight_part = jnp.einsum("to,tf->of", dbranch, active, preferred_element_type=f32)
    dactive = jnp.dot(dbranch, outer_full, preferred_element_type=f32)
    unused, gelu_pull = jax.vjp(exact_gelu, hidden)
    dhidden = gelu_pull(dactive)[0].astype(jnp.bfloat16)
    inner_weight_part = jnp.einsum("td,tf->df", normed_low, dhidden, preferred_element_type=f32)
    inner_bias_part = jnp.sum(dhidden.astype(f32), 0)
    dnormed_part = jnp.einsum("tf,df->td", dhidden, inner_full, preferred_element_type=f32)
    dnormed = dres_second + tp_sum(dnormed_part)
    dres_first, attn_gain_part, attn_shift_part = norm_back(
        dnormed, normal_first, inverse_first, gain_first
    )
    dattended = dres_first.astype(jnp.bfloat16)
    output_bias_part = jnp.sum(dattended.astype(f32), 0)
    output_weight_part = jnp.einsum("to,th->oh", dattended, context, preferred_element_type=f32)
    dcontext = jnp.dot(dattended, output_full, preferred_element_type=f32).astype(jnp.bfloat16)

    rest_piece = lax.psum(
        lax.psum_scatter(
            jnp.concatenate([output_weight_part, inner_weight_part, outer_weight_part], axis=1),
            "shard", scatter_dimension=0, tiled=True,
        ),
        "ctx",
    )
    output_total = rest_piece[:, :head_width]
    inner_total = rest_piece[:, head_width : head_width + hidden_width]
    outer_total = rest_piece[:, head_width + hidden_width :]

    def head_backward(quintet):
        query_head, key_head, value_head, dcontext_head, log_sum = quintet
        portion = jnp.exp(scores_of(query_head, key_head) - log_sum[:, None])
        dportion = jnp.einsum("qd,kd->qk", dcontext_head, value_head, preferred_element_type=f32)
        dvalue_head = jnp.einsum(
            "qk,qd->kd", portion.astype(jnp.bfloat16), dcontext_head, preferred_element_type=f32
        )
        centering = jnp.sum(portion * dportion, -1, keepdims=True)
        dscores = (portion * (dportion - centering)).astype(jnp.bfloat16)
        dquery_head = jnp.dot(dscores, key_head, preferred_element_type=f32) * factor
        dkey_head = (
            jnp.einsum("qk,qd->kd", dscores, query_head, preferred_element_type=f32) * factor
        )
        return (dquery_head.astype(jnp.bfloat16), dkey_head, dvalue_head)

    dquery_heads, dkey_heads, dvalue_heads = lax.map(
        head_backward, (query_heads, key_heads, value_heads, split_heads(dcontext), log_sums)
    )
    dquery = join_heads(dquery_heads)
    dkv = lax.psum_scatter(
        jnp.concatenate([join_heads(dkey_heads), join_heads(dvalue_heads)], axis=1),
        "ctx", scatter_dimension=0, tiled=True,
    ).astype(jnp.bfloat16)
    dkeys = dkv[:, :head_width]
    dvalues = dkv[:, head_width:]
    dqkv = jnp.concatenate([dquery, dkeys, dvalues], axis=1)
    qkv_weight_part = jnp.einsum("td,th->dh", tokens, dqkv, preferred_element_type=f32)
    query_bias_part = jnp.sum(dquery.astype(f32), 0)
    value_bias_part = jnp.sum(dvalues.astype(f32), 0)
    dinput_part = jnp.einsum("th,dh->td", dqkv, qkv_full, preferred_element_type=f32)
    tokens_gradient = dres_first + tp_sum(dinput_part)
    qkv_piece = lax.psum(
        lax.psum_scatter(qkv_weight_part, "shard", scatter_dimension=0, tiled=True), "ctx"
    )
    query_total = qkv_piece[:, :head_width]
    key_total = qkv_piece[:, head_width : 2 * head_width]
    value_total = qkv_piece[:, 2 * head_width :]

    first_core = (tensor_place == 0).astype(f32)
    spread = lambda part, width: lax.dynamic_update_slice_in_dim(
        jnp.zeros((width * tensor_count,), f32), part, tensor_place * width, 0
    )
    vector_parts = jnp.concatenate(
        [
            first_core * jnp.stack(
                [output_bias_part, attn_gain_part, attn_shift_part, outer_bias_part,
                 final_gain_part, final_shift_part]
            ).reshape(-1),
            spread(query_bias_part, head_width),
            spread(value_bias_part, head_width),
            spread(inner_bias_part, hidden_width),
        ]
    )
    vector_sums = lax.psum(vector_parts, ("shard", "ctx", "tp"))
    shard_place = lax.axis_index("shard")
    shard_sums = vector_sums[: 6 * model_width].reshape(6, model_width)
    shard_sums = lax.dynamic_slice_in_dim(shard_sums, shard_place * piece, piece, 1)
    outbias_total, attn_gain_total, attn_shift_total, outerbias_total, final_gain_total, final_shift_total = shard_sums
    block = shard_place * tensor_count + tensor_place
    start = 6 * model_width
    qbias_total = lax.dynamic_slice_in_dim(vector_sums, start + block * qb, qb)
    vbias_total = lax.dynamic_slice_in_dim(vector_sums, start + model_width + block * qb, qb)
    ibias_total = lax.dynamic_slice_in_dim(vector_sums, start + 2 * model_width + block * ib, ib)
    return (
        layer_out,
        tokens_gradient,
        query_total,
        qbias_total,
        key_total,
        value_total,
        vbias_total,
        output_total,
        outbias_total,
        attn_gain_total,
        attn_shift_total,
        inner_total,
        ibias_total,
        outer_total,
        outerbias_total,
        final_gain_total,
        final_shift_total,
    )


def solution(mesh):
    placed = (
        P(("shard", "ctx"), None),
        P("shard"),
        P("shard", "tp"),
        P(("shard", "tp")),
        P("shard", "tp"),
        P("shard", "tp"),
        P(("shard", "tp")),
        P("shard", "tp"),
        P("shard"),
        P("shard"),
        P("shard"),
        P("shard", "tp"),
        P(("shard", "tp")),
        P("shard", "tp"),
        P("shard"),
        P("shard"),
        P("shard"),
        P(("shard", "ctx"), None),
    )
    return jax.shard_map(
        on_device,
        mesh=mesh,
        in_specs=placed,
        out_specs=(
            P(("shard", "ctx"), None),
            P(("shard", "ctx"), None),
            P("shard", "tp"),
            P(("shard", "tp")),
            P("shard", "tp"),
            P("shard", "tp"),
            P(("shard", "tp")),
            P("shard", "tp"),
            P("shard"),
            P("shard"),
            P("shard"),
            P("shard", "tp"),
            P(("shard", "tp")),
            P("shard", "tp"),
            P("shard"),
            P("shard"),
            P("shard"),
        ),
        check_vma=False,
    )
```

time: 1050 us -> 816 us (0.78)
  waiting for transfers between devices: 593 us -> 454 us
  blocking collectives: 132 us -> 70.1 us
  matrix products: 180 us -> 159 us
  other arithmetic: 42 us -> 59 us
  local copies, waits for them, and re-layouts: 66.1 us -> 51 us
    psum x5 -> x1, waiting for transfers between devices: 153 us -> 91.3 us  [on_device(): lax.psum(lax.psum_scatter(qkv_weight_part, 'shard', scatter_dimension=0,...]
    reduce_scatter x5 -> x2, waiting for transfers between devices: 292 us -> 240 us  [the longest x1 135 us: on_device(): lax.psum_scatter(jnp.concatenate([join_heads(dkey_heads), join_heads(dval...]
    all_gather x5 -> x0, blocking collectives: 50.8 us -> none  [the longest x1 12.4 us: on_device(): lax.all_gather(value_weight, 'shard', axis=0, tiled=True)]
    unnamed x4 -> x1, blocking collectives: 67.1 us -> 26.7 us
    unnamed x20 -> x8, waiting for transfers between devices: 68.9 us -> 35.9 us
    psum x1, blocking collectives: 14.1 us -> 43.4 us  [on_device(): vector_sums = lax.psum(vector_parts, ('shard', 'ctx', 'tp'))]
    unnamed x132 -> x72, local copies, waits for them, and re-layouts: 36.5 us -> 13.3 us
    dot_general x48 -> x42, matrix products: 152 us -> 131 us  [the longest x12 32.5 us: scores_of(): jnp.einsum('qd,kd->qk', query_head, key_head, preferred_element_type=f32)]
  transfers between devices with their start and end apart: 17 -> 11, of which waited for: 15 -> 9; matrix products, arithmetic and copies ran while one was open for 7% -> 13% of each run, Pallas kernels for 0% -> 0%
where the time goes in v1:
time: 816 us; the launch traced here: 810 us
  waiting for transfers between devices  454 us (56%)
  matrix products  159 us (19%)
  blocking collectives  70.1 us (9%)
  other arithmetic  59 us (7%)
  local copies, waits for them, and re-layouts  51 us (6%)
  between operations  15.6 us (2%)
    reduce_scatter x1, waiting for transfers between devices, on_device(): lax.psum_scatter(jnp.concatenate([join_heads(dkey_heads), join_heads(dval...  135 us
    reduce_scatter x1, waiting for transfers between devices, on_device(): lax.psum_scatter(jnp.concatenate([output_weight_part, inner_weight_part,...  105 us
    psum x1, waiting for transfers between devices, on_device(): lax.psum(lax.psum_scatter(qkv_weight_part, 'shard', scatter_dimension=0,...  91.3 us
    all_gather x1, waiting for transfers between devices, on_device(): lax.all_gather(jnp.concatenate([key_local, value_local], axis=1), 'ctx',...  74.7 us
    psum x1, blocking collectives, on_device(): vector_sums = lax.psum(vector_parts, ('shard', 'ctx', 'tp'))  43.4 us
    unnamed x8, waiting for transfers between devices  35.9 us
    dot_general x12, matrix products, scores_of(): jnp.einsum('qd,kd->qk', query_head, key_head, preferred_element_type=f32)  32.5 us
    dot_general x6, matrix products, head_forward(): mixed = jnp.dot(portion, value_head, preferred_element_type=f32)  28.1 us
  transfers between devices with their start and end apart: 11, of which 9 were waited for; matrix products, arithmetic and copies ran while one was open for 13% of the time, Pallas kernels for 0%

profile of v1, /device:TPU:0, one launch (start us, length us, event | category | flops | bytes accessed | tf_op | source)
XLA Modules:
  0.0 810.4 jit_solution(7573852430526426524)
XLA Ops:
  11.1 6.1 concatenate.26
  17.5 26.7 %all-reduce = bf16[13824]{0:T(1024)(128)(2,1)S(1)} all-reduce(bf16[13824]{0:T(1024)(128)(2,1)S(1)} %dynamic-update-slice), channel_id=2, replica_groups=mesh['shard'=4,'ctx'=4,'tp'=2] {'shard','tp'}, use_global_device_ids=true, to_apply=%add | all-reduce | flops 13824 | bytes 55296
  52.5 74.7 %all-gather.7.cloned.1.call-done = bf16[2560,768]{0,1:T(8,128)(2,1)} async-done(((bf16[640,768]{0,1:T(8,128)(2,1)}), bf16[2560,768]{0,1:T(8,128)(2,1)}) %all-gather.7.cloned.1.call-update) | async-done | bytes 3932176 | tf_op jit(solution)/shard_map/all_gather | solution.py:103
  130.9 4.9 copy.52
  138.9 62.6 %while.28 = (s32[]{:T(128)}, bf16[6,640,64]{1,2,0:T(8,128)(2,1)S(1)}, f32[6,640]{1,0:T(8,128)S(1)}, bf16[6,640,64]{2,1,0:T(8,128)(2,1)S(1)}, bf16[6,2560,64]{2,1...) while((s32[]{:T(128)}, ...), condition=%wide.region_3.4_spmd.clone, body=%wide.region_0.3_spmd.clone.sunk | while | flops 439134080 | bytes 47478912 | solution.py:136
  144.7 4.7 fusion.130
  155.1 4.7 fusion.130
  165.6 4.7 fusion.130
  176.0 4.7 fusion.130
  186.4 4.7 fusion.130
  196.9 4.7 fusion.130
  211.6 12.0 %multiply_convert_fusion.1 = (bf16[640,1536]{1,0:T(8,128)(2,1)S(1)}, f32[640,1536]{1,0:T(8,128)}, f32[640,1536]{1,0:T(8,128)}) fusion(f32[1536]{0:T(1024)S(1)} %dynamic-slice_convert_fusion, bf16[768,3456]{1,0:T(8,128)(2,1)S(1)} %copy-done.16, f32[640,768]{1,0:T(8,128)S(1)} %get-tuple-element.265, f32[768]{0:T(1024)S(1)} %add.179, f32[768]{0:T(1024)S(1)} %mul.180, ...), kind=kOutput, calls=%fused_computation.65 | convolution fusion | flops 1577287680 | bytes 14180352 | tf_op jit(solution)/shard_map/dot_general | solution.py:143
  245.3 4.2 collective-permute-done.2
  249.4 4.4 multiply_reduce_fusion.1
  260.3 82.1 %while.29 = (s32[]{:T(128)}, bf16[6,640,64]{1,2,0:T(8,128)(2,1)}, f32[6,2560,64]{1,2,0:T(8,128)}, f32[6,2560,64]{1,2,0:T(8,128)}, bf16[6,640,64]{2,1,0:T(8,128)(...) while((s32[]{:T(128)}, bf16[6,640,64]{1,2,0:T(8,128)(2,1)}, ...), condition=%wide.region_14.15_spmd.clone, body=%wide.region_12.14_spmd.clone.sunk | while | flops 1063569280 | bytes 53191284 | solution.py:197
  342.5 6.9 pad_maximum_fusion.1
  349.4 135.1 %reduce-scatter.6.cloned.1.call-done = f32[640,768]{0,1:T(8,128)} async-done(((f32[2560,768]{0,1:T(8,128)}), f32[640,768]{0,1:T(8,128)}) %reduce-scatter.6.cloned.1.call-update) | async-done | bytes 1966096 | tf_op jit(solution)/shard_map/reduce_scatter | solution.py:201
  493.1 4.3 fusion.83
  500.5 4.4 pad_maximum_fusion
  505.0 35.8 %reduce-scatter.10.cloned.1.call-done = f32[192,1152]{1,0:T(8,128)} async-done(((f32[768,1152]{1,0:T(8,128)}), f32[192,1152]{1,0:T(8,128)}) %reduce-scatter.10.cloned.1.call-update) | async-done | bytes 884752
  543.4 105.0 %reduce-scatter.8.cloned.1.call-done = f32[192,3456]{1,0:T(8,128)} async-done(((f32[768,3456]{1,0:T(8,128)}), f32[192,3456]{1,0:T(8,128)}) %reduce-scatter.8.cloned.1.call-update) | async-done | bytes 2654224 | tf_op jit(solution)/shard_map/reduce_scatter | solution.py:172
  648.5 4.5 fusion.74
  655.3 43.4 %psum.22 = f32[9216]{0:T(1024)S(1)} all-reduce(f32[9216]{0:T(1024)S(1)} %pad_maximum_fusion.8), channel_id=1, replica_groups=mesh['shard'=4,'ctx'=4,'tp'=2] {'shard','ctx','tp'}, use_global_device_ids=true, to_apply=%region_27.28 | all-reduce | flops 9216 | bytes 73728 | tf_op jit(solution)/shard_map/psum | solution.py:235
  704.5 91.3 %all-reduce.4.cloned.1.call-done = (f32[192,1152]{0,1:T(8,128)}, f32[192,3456]{1,0:T(8,128)}) async-done(((f32[192,1152]{0,1:T(8,128)}, f32[192,3456]{1,0:T(8,128)}), (f32[192,1152]{0,1:T(8,128)}, f32[192,3456]{1,0:T(8,128)})) %all-reduce.4.cloned.1.call-update) | async-done | bytes 3538960 | tf_op jit(solution)/shard_map/psum | solution.py:213
  (276 shorter events, 202.2 us)
Async XLA Ops:
  7.2 38.8 %all-gather.5.cloned.1.call-start = ((), (), s32[]{:S(2)}) async-start(), calls=%async_computation.3 | async-start | bytes 2211840 | tf_op jit(solution)/shard_map/all_gather | solution.py:67
  9.1 118.1 %all-gather.7.cloned.1.call-start = ((), (), s32[]{:S(2)}) async-start(), calls=%async_computation.4 | async-start | bytes 4915200 | tf_op jit(solution)/shard_map/all_gather | solution.py:103
  50.6 151.0 %all-gather.9.cloned.1.call-start = ((), (), s32[]{:S(2)}) async-start(), calls=%async_computation.5 | async-start | bytes 6635520 | tf_op jit(solution)/shard_map/all_gather | solution.py:74
  51.9 432.6 %reduce-scatter.6.cloned.1.call-start = ((), (), s32[]{:S(2)}) async-start(), calls=%async_computation.6 | async-start | bytes 9830400 | tf_op jit(solution)/shard_map/reduce_scatter | solution.py:201
  204.3 4.2 collective-permute-start
  204.9 26.0 %copy-start.22 = (f32[768]{0:T(1024)}, f32[768]{0:T(1024)S(1)}, u32[]{:S(2)}) copy-start(f32[768]{0:T(1024)S(1)} %add.179) | copy-start | bytes 9220
  205.5 6.1 copy-start.16
  211.2 42.6 %copy-start.1 = (f32[640,768]{1,0:T(8,128)}, f32[640,768]{1,0:T(8,128)S(1)}, u32[]{:S(2)}) copy-start(f32[640,768]{1,0:T(8,128)S(1)} %get-tuple-element.265) | copy-start | bytes 5898244
  226.6 4.3 collective-permute-start.1
  227.0 7.3 copy-start.10
  230.9 7.5 slice-start
  245.1 4.3 collective-permute-start.2
  349.4 191.4 %reduce-scatter.10.cloned.1.call-start = ((), (), s32[]{:S(2)}) async-start(), calls=%async_computation.8 | async-start | bytes 4423680
  493.0 155.3 %reduce-scatter.8.cloned.1.call-start = ((), (), s32[]{:S(2)}) async-start(), calls=%async_computation.7 | async-start | bytes 13271040 | tf_op jit(solution)/shard_map/reduce_scatter | solution.py:172
  505.0 143.4 %copy-start.12 = (bf16[640,768]{0,1:T(8,128)(2,1)S(1)}, bf16[640,768]{0,1:T(8,128)(2,1)}, u32[]{:S(2)}) copy-start(bf16[640,768]{0,1:T(8,128)(2,1)} %copy-done.11) | copy-start | bytes 2949124
  505.0 290.8 %all-reduce.4.cloned.1.call-start = ((), (), s32[]{:S(2)}) async-start(), calls=%async_computation.9 | async-start | bytes 7667712 | tf_op jit(solution)/shard_map/psum | solution.py:213
  648.4 4.6 copy-start.19
  648.4 4.6 copy-start.25
  648.4 5.0 copy-start.24
  648.4 5.0 copy-start.21
  648.4 5.0 copy-start.20
  648.4 52.3 %copy-start.5 = (f32[640,768]{1,0:T(8,128)S(1)}, f32[640,768]{1,0:T(8,128)}, u32[]{:S(2)}) copy-start(f32[640,768]{1,0:T(8,128)} %copy-done.3) | copy-start | bytes 5898244
  653.0 47.7 %collective-permute-start.3 = (f32[640,768]{1,0:T(8,128)}, f32[640,768]{1,0:T(8,128)}, u32[]{:S(2)}, u32[]{:S(2)}) collective-permute-start(f32[640,768]{1,0:T(8,128)} %fusion.74), channel_id=1, source_target_pairs={{0,1},{1,0},{2,3},{3,2},{4,5},{5,4},{6,7},{7,6},{8,9},{9,8},{10,11... | collective-permute-start | bytes 5898248 | tf_op jit(solution)/shard_map/ppermute | solution.py:34
  795.7 5.0 copy-start.13
  (25 other events, 68.1 us)
Sparse Core Ops, SparseCore 0:
  10.4 35.4 all-gather.4
  50.7 76.4 all-gather.6
  129.0 60.3 all-gather.8
  349.5 134.9 reduce-scatter.5
  493.1 47.6 reduce-scatter.9
  543.8 104.5 reduce-scatter.7
  651.4 144.3 all-reduce.3

commit v2 on v1

--- a/solution.py
+++ b/solution.py
@@ -33,6 +33,14 @@
     if lax.axis_size("tp") == 2:
         return value + lax.ppermute(value, "tp", [(0, 1), (1, 0)])
     return lax.psum(value, "tp")
+
+
+def tp_gather(value):
+    if lax.axis_size("tp") == 2:
+        other = lax.ppermute(value, "tp", [(0, 1), (1, 0)])
+        first = lax.axis_index("tp") == 0
+        return jnp.stack([jnp.where(first, value, other), jnp.where(first, other, value)])
+    return lax.all_gather(value, "tp")
 
 
 def on_device(
@@ -64,10 +72,29 @@
     factor = HEAD_DIM ** (-0.5)
     f32 = jnp.float32
 
+    qb = query_bias.shape[0]
+    ib = inner_bias.shape[0]
+    piece = output_bias.shape[0]
+    tp_blocks = tp_gather(jnp.concatenate([query_bias, value_bias, inner_bias]))
+    bias_columns = jnp.concatenate(
+        [
+            tp_blocks[:, :qb].reshape(piece, 1),
+            tp_blocks[:, qb : 2 * qb].reshape(piece, 1),
+            tp_blocks[:, 2 * qb :].reshape(piece, -1),
+        ],
+        axis=1,
+    )
+    shard_columns = jnp.stack(
+        [output_bias, attn_gain, attn_shift, outer_bias, final_gain, final_shift], axis=1
+    )
     qkv_full = lax.all_gather(
-        jnp.concatenate([query_weight, key_weight, value_weight], axis=1),
+        jnp.concatenate(
+            [query_weight, key_weight, value_weight, shard_columns, bias_columns], axis=1
+        ),
         "shard", axis=0, tiled=True,
     )
+    vector_full = qkv_full[:, 3 * head_width :]
+    qkv_full = qkv_full[:, : 3 * head_width]
     query_full = qkv_full[:, :head_width]
     key_full = qkv_full[:, head_width : 2 * head_width]
     value_full = qkv_full[:, 2 * head_width :]
@@ -79,19 +106,11 @@
     inner_full = rest_full[:, head_width : head_width + hidden_width]
     outer_full = rest_full[:, head_width + hidden_width :]
 
-    shard_vectors = (output_bias, attn_gain, attn_shift, outer_bias, final_gain, final_shift)
-    piece = output_bias.shape[0]
-    packed = jnp.concatenate(shard_vectors + (query_bias, value_bias, inner_bias))
-    gathered = lax.all_gather(packed, ("shard", "tp"), axis=0)
-    by_shard = gathered[::tensor_count, : 6 * piece].reshape(-1, 6, piece)
-    full_vectors = by_shard.transpose(1, 0, 2).reshape(6, -1).astype(f32)
+    full_vectors = vector_full[:, :6].T.astype(f32)
     outbias_full, gain_first, shift_first, outerbias_full, gain_second, shift_second = full_vectors
-    offset = 6 * piece
-    qb = query_bias.shape[0]
-    ib = inner_bias.shape[0]
-    qbias_all = gathered[:, offset : offset + qb].reshape(-1)
-    vbias_all = gathered[:, offset + qb : offset + 2 * qb].reshape(-1)
-    ibias_all = gathered[:, offset + 2 * qb : offset + 2 * qb + ib].reshape(-1)
+    qbias_all = vector_full[:, 6]
+    vbias_all = vector_full[:, 7]
+    ibias_all = vector_full[:, 8:].reshape(-1)
     query_shift = lax.dynamic_slice_in_dim(qbias_all, tensor_place * head_width, head_width).astype(f32)
     value_shift = lax.dynamic_slice_in_dim(vbias_all, tensor_place * head_width, head_width).astype(f32)
     inner_shift = lax.dynamic_slice_in_dim(ibias_all, tensor_place * hidden_width, hidden_width).astype(f32)
@@ -168,16 +187,37 @@
     output_weight_part = jnp.einsum("to,th->oh", dattended, context, preferred_element_type=f32)
     dcontext = jnp.dot(dattended, output_full, preferred_element_type=f32).astype(jnp.bfloat16)
 
-    rest_piece = lax.psum(
-        lax.psum_scatter(
-            jnp.concatenate([output_weight_part, inner_weight_part, outer_weight_part], axis=1),
-            "shard", scatter_dimension=0, tiled=True,
-        ),
-        "ctx",
-    )
-    output_total = rest_piece[:, :head_width]
-    inner_total = rest_piece[:, head_width : head_width + hidden_width]
-    outer_total = rest_piece[:, head_width + hidden_width :]
+    low = jnp.bfloat16
+    rows = model_width
+    early = jnp.concatenate(
+        [
+            output_weight_part,
+            inner_weight_part,
+            outer_weight_part,
+            jnp.stack(
+                [output_bias_part, attn_gain_part, attn_shift_part, outer_bias_part,
+                 final_gain_part, final_shift_part],
+                axis=1,
+            ),
+            tp_gather(inner_bias_part).reshape(rows, -1),
+        ],
+        axis=1,
+    ).astype(low)
+    early, dcontext = lax.optimization_barrier((early, dcontext))
+    early_piece = lax.psum(
+        lax.psum_scatter(early, "shard", scatter_dimension=0, tiled=True), "ctx"
+    ).astype(f32)
+    output_total = early_piece[:, :head_width]
+    inner_total = early_piece[:, head_width : head_width + hidden_width]
+    outer_total = early_piece[:, head_width + hidden_width : head_width + 2 * hidden_width]
+    early_vectors = early_piece[:, head_width + 2 * hidden_width :]
+    outbias_total, attn_gain_total, attn_shift_total, outerbias_total, final_gain_total, final_shift_total = (
+        early_vectors[:, :6].T
+    )
+    local_rows = piece // tensor_count
+    ibias_total = lax.dynamic_slice_in_dim(
+        early_vectors[:, 6:], tensor_place * local_rows, local_rows, 0
+    ).reshape(-1)
 
     def head_backward(quintet):
         query_head, key_head, value_head, dcontext_head, log_sum = quintet
@@ -199,7 +239,7 @@
     )
     dquery = join_heads(dquery_heads)
     dkv = lax.psum_scatter(
-        jnp.concatenate([join_heads(dkey_heads), join_heads(dvalue_heads)], axis=1),
+        jnp.concatenate([join_heads(dkey_heads), join_heads(dvalue_heads)], axis=1).astype(low),
         "ctx", scatter_dimension=0, tiled=True,
     ).astype(jnp.bfloat16)
     dkeys = dkv[:, :head_width]
@@ -210,38 +250,26 @@
     value_bias_part = jnp.sum(dvalues.astype(f32), 0)
     dinput_part = jnp.einsum("th,dh->td", dqkv, qkv_full, preferred_element_type=f32)
     tokens_gradient = dres_first + tp_sum(dinput_part)
-    qkv_piece = lax.psum(
-        lax.psum_scatter(qkv_weight_part, "shard", scatter_dimension=0, tiled=True), "ctx"
-    )
-    query_total = qkv_piece[:, :head_width]
-    key_total = qkv_piece[:, head_width : 2 * head_width]
-    value_total = qkv_piece[:, 2 * head_width :]
-
-    first_core = (tensor_place == 0).astype(f32)
-    spread = lambda part, width: lax.dynamic_update_slice_in_dim(
-        jnp.zeros((width * tensor_count,), f32), part, tensor_place * width, 0
-    )
-    vector_parts = jnp.concatenate(
+    late = jnp.concatenate(
         [
-            first_core * jnp.stack(
-                [output_bias_part, attn_gain_part, attn_shift_part, outer_bias_part,
-                 final_gain_part, final_shift_part]
-            ).reshape(-1),
-            spread(query_bias_part, head_width),
-            spread(value_bias_part, head_width),
-            spread(inner_bias_part, hidden_width),
-        ]
-    )
-    vector_sums = lax.psum(vector_parts, ("shard", "ctx", "tp"))
-    shard_place = lax.axis_index("shard")
-    shard_sums = vector_sums[: 6 * model_width].reshape(6, model_width)
-    shard_sums = lax.dynamic_slice_in_dim(shard_sums, shard_place * piece, piece, 1)
-    outbias_total, attn_gain_total, attn_shift_total, outerbias_total, final_gain_total, final_shift_total = shard_sums
-    block = shard_place * tensor_count + tensor_place
-    start = 6 * model_width
-    qbias_total = lax.dynamic_slice_in_dim(vector_sums, start + block * qb, qb)
-    vbias_total = lax.dynamic_slice_in_dim(vector_sums, start + model_width + block * qb, qb)
-    ibias_total = lax.dynamic_slice_in_dim(vector_sums, start + 2 * model_width + block * ib, ib)
+            qkv_weight_part,
+            tp_gather(query_bias_part).reshape(rows, 1),
+            tp_gather(value_bias_part).reshape(rows, 1),
+        ],
+        axis=1,
+    ).astype(low)
+    late_piece = lax.psum(
+        lax.psum_scatter(late, "shard", scatter_dimension=0, tiled=True), "ctx"
+    ).astype(f32)
+    query_total = late_piece[:, :head_width]
+    key_total = late_piece[:, head_width : 2 * head_width]
+    value_total = late_piece[:, 2 * head_width : 3 * head_width]
+    qbias_total = lax.dynamic_slice_in_dim(
+        late_piece[:, 3 * head_width], tensor_place * local_rows, local_rows
+    )
+    vbias_total = lax.dynamic_slice_in_dim(
+        late_piece[:, 3 * head_width + 1], tensor_place * local_rows, local_rows
+    )
     return (
         layer_out,
         tokens_gradient,

time: 816 us -> 675 us (0.83)
  waiting for transfers between devices: 454 us -> 362 us
  blocking collectives: 70.1 us -> 0 us
  local copies, waits for them, and re-layouts: 51 us -> 82 us
  other arithmetic: 59 us -> 47.1 us
    reduce_scatter x2 -> x1, waiting for transfers between devices: 240 us -> 64.3 us  [on_device(): lax.psum_scatter(early, 'shard', scatter_dimension=0, tiled=True)]
    unnamed x8 -> x9, waiting for transfers between devices: 35.9 us -> 99 us
    psum x1 -> x0, blocking collectives: 43.4 us -> none  [on_device(): vector_sums = lax.psum(vector_parts, ('shard', 'ctx', 'tp'))]
    all_gather x1, waiting for transfers between devices: 1.35 us -> 36.6 us  [on_device(): lax.all_gather(jnp.concatenate([query_weight, key_weight, value_weight, s...]
    unnamed x1 -> x0, blocking collectives: 26.7 us -> none
    concatenate x1 -> x3, local copies, waits for them, and re-layouts: 6.12 us -> 18.9 us  [the longest x1 9.69 us: on_device(): jnp.concatenate([output_weight_part, inner_weight_part, outer_weight_part...]
    psum x1, waiting for transfers between devices: 91.3 us -> 81.9 us  [on_device(): lax.psum(lax.psum_scatter(late, 'shard', scatter_dimension=0, tiled=True)...]
    unnamed x72 -> x53, local copies, waits for them, and re-layouts: 13.3 us -> 20.1 us
  transfers between devices with their start and end apart: 11 -> 15, of which waited for: 9 -> 9; matrix products, arithmetic and copies ran while one was open for 13% -> 15% of each run, Pallas kernels for 0% -> 0%
where the time goes in v2:
time: 675 us; the launch traced here: 666 us
  waiting for transfers between devices  362 us (54%)
  matrix products  157 us (23%)
  local copies, waits for them, and re-layouts  82 us (12%)
  other arithmetic  47.1 us (7%)
  between operations  14.9 us (2%)
    unnamed x9, waiting for transfers between devices  99 us
    psum x1, waiting for transfers between devices, on_device(): lax.psum(lax.psum_scatter(late, 'shard', scatter_dimension=0, tiled=True)...  81.9 us
    all_gather x1, waiting for transfers between devices, on_device(): lax.all_gather(jnp.concatenate([key_local, value_local], axis=1), 'ctx',...  74.6 us
    reduce_scatter x1, waiting for transfers between devices, on_device(): lax.psum_scatter(early, 'shard', scatter_dimension=0, tiled=True)  64.3 us
    all_gather x1, waiting for transfers between devices, on_device(): lax.all_gather(jnp.concatenate([query_weight, key_weight, value_weight, s...  36.6 us
    dot_general x12, matrix products, scores_of(): jnp.einsum('qd,kd->qk', query_head, key_head, preferred_element_type=f32)  32.5 us
    dot_general x6, matrix products, head_forward(): mixed = jnp.dot(portion, value_head, preferred_element_type=f32)  28.1 us
    unnamed x53, local copies, waits for them, and re-layouts  20.1 us
  transfers between devices with their start and end apart: 15, of which 9 were waited for; matrix products, arithmetic and copies ran while one was open for 15% of the time, Pallas kernels for 0%

profile of v2, /device:TPU:0, one launch (start us, length us, event | category | flops | bytes accessed | tf_op | source)
XLA Modules:
  0.0 665.9 jit_solution(18350273729721554385)
XLA Ops:
  16.5 36.6 %all-gather.4.cloned.1.call-done = bf16[768,1164]{1,0:T(8,128)(2,1)} async-done(((bf16[192,1164]{1,0:T(8,128)(2,1)}), bf16[768,1164]{1,0:T(8,128)(2,1)}) %all-gather.4.cloned.1.call-update) | async-done | bytes 1787920 | tf_op jit(solution)/shard_map/all_gather | solution.py:90
  61.1 74.6 %all-gather.6.cloned.1.call-done = bf16[2560,768]{0,1:T(8,128)(2,1)} async-done(((bf16[640,768]{0,1:T(8,128)(2,1)}), bf16[2560,768]{0,1:T(8,128)(2,1)}) %all-gather.6.cloned.1.call-update) | async-done | bytes 3932176 | tf_op jit(solution)/shard_map/all_gather | solution.py:122
  139.4 4.8 copy.75
  147.3 62.9 %while.28 = (s32[]{:T(128)}, bf16[6,640,64]{1,2,0:T(8,128)(2,1)S(1)}, f32[6,640]{1,0:T(8,128)S(1)}, bf16[6,640,64]{2,1,0:T(8,128)(2,1)S(1)}, bf16[6,2560,64]{2,1...) while((s32[]{:T(128)}, ...), condition=%wide.region_3.4_spmd.clone, body=%wide.region_0.3_spmd.clone.sunk | while | flops 439134080 | bytes 47478912 | solution.py:155
  153.1 4.7 fusion.129
  163.5 4.7 fusion.129
  174.0 4.7 fusion.129
  184.4 4.7 fusion.129
  194.9 4.7 fusion.129
  205.3 4.7 fusion.129
  220.2 10.2 %multiply_convert_fusion.1 = (bf16[640,1536]{1,0:T(8,128)(2,1)S(1)}, f32[640,1536]{1,0:T(8,128)S(1)}, f32[640,1536]{1,0:T(8,128)S(1)}) fusion(f32[1536]{0:T(1024)S(1)} %dynamic-slice_convert_fusion, bf16[768,3456]{1,0:T(8,128)(2,1)S(1)} %bitcast.155, f32[640,768]{1,0:T(8,128)S(1)} %get-tuple-element.294, f32[768]{0:T(1024)S(1)} %get-tuple-element.239, ...), kind=kOutput, calls=%fused_computation.64 | convolution fusion | flops 1577287680 | bytes 14180352 | tf_op jit(solution)/shard_map/dot_general | solution.py:162
  233.6 3.9 collective-permute-done.2
  248.6 5.4 convolution_convert_fusion.2
  259.9 3.8 multiply_reduce_fusion.1
  269.9 9.7 %concatenate.32 = bf16[768,3466]{1,0:T(8,128)(2,1)} concatenate(bf16[768,384]{1,0:T(8,128)(2,1)} %copy.77, bf16[768,1536]{1,0:T(8,128)(2,1)} %convolution_convert_fusion.2, bf16[768,1536]{1,0:T(8,128)(2,1)} %convolution_convert_fusion.1, bf16[768,1]{1,0:T(8,128)(2,1)} %stack.117, bf16[768,1]{1,0:T(8,128)(2,1)} %stack.118, bf16[768,1]{1,0:T(8,128)(2,1)} %stack.119, ...), dimensions={1} | concatenate | bytes 10647552 | tf_op jit(solution)/shard_map/concatenate | solution.py:192
  284.2 81.5 %while.29 = (s32[]{:T(128)}, bf16[6,640,64]{1,2,0:T(8,128)(2,1)}, bf16[6,2560,64]{1,2,0:T(8,128)(2,1)}, bf16[6,2560,64]{1,2,0:T(8,128)(2,1)}, bf16[6,640,64]{2,1...) while((s32[]{:T(128)}, bf16[6,640,64]{1,2,0:T(8,128)(2,1)}, ...), condition=%wide.region_21.22_spmd.clone, body=%wide.region_19.21_spmd.clone.sunk | while | flops 1063569280 | bytes 56959660 | solution.py:237
  365.8 4.3 pad_maximum_fusion
  370.1 6.3 copy.89
  378.9 69.0 %reduce-scatter.10.cloned.1.call-done = bf16[640,768]{1,0:T(8,128)(2,1)} async-done(((bf16[2560,768]{1,0:T(8,128)(2,1)}), bf16[640,768]{1,0:T(8,128)(2,1)}) %reduce-scatter.10.cloned.1.call-update) | async-done | bytes 983056
  452.5 7.2 %concatenate.35 = bf16[768,1154]{0,1:T(8,128)(2,1)S(1)} concatenate(bf16[768,1152]{0,1:T(8,128)(2,1)} %fusion.54, bf16[768,1]{0,1:T(2,128)(2,1)S(1)} %bitcast.156, bf16[768,1]{0,1:T(2,128)(2,1)S(1)} %bitcast.157), dimensions={1} | concatenate | bytes 3545088 | tf_op jit(solution)/shard_map/concatenate | solution.py:253
  462.7 4.3 fusion.73
  467.5 29.4 %reduce-scatter.12.cloned.1.call-done = bf16[192,1154]{1,0:T(8,128)(2,1)} async-done(((bf16[768,1154]{1,0:T(8,128)(2,1)}), bf16[192,1154]{1,0:T(8,128)(2,1)}) %reduce-scatter.12.cloned.1.call-update) | async-done | bytes 443152
  499.0 64.3 %reduce-scatter.8.cloned.1.call-done = bf16[192,3466]{1,0:T(8,128)(2,1)} async-done(((bf16[768,3466]{1,0:T(8,128)(2,1)}), bf16[192,3466]{1,0:T(8,128)(2,1)}) %reduce-scatter.8.cloned.1.call-update) | async-done | bytes 1330960 | tf_op jit(solution)/shard_map/reduce_scatter | solution.py:208
  567.1 81.9 %all-reduce.3.cloned.1.call-done = (bf16[192,1154]{0,1:T(8,128)(2,1)}, bf16[192,3466]{1,0:T(8,128)(2,1)}) async-done(((bf16[192,1154]{0,1:T(8,128)(2,1)}, bf16[192,3466]{1,0:T(8,128)(2,1)}), (bf16[192,1154]{0,1:T(8,128)(2,1)}, bf16[192,3466]{1,0:T(8,128)(2,1)})) %all-reduce.3.cloned.1.call-update) | async-done | bytes 1774096 | tf_op jit(solution)/shard_map/psum | solution.py:261
  (299 shorter events, 206.3 us)
Async XLA Ops:
  7.2 45.9 %all-gather.4.cloned.1.call-start = ((), (), s32[]{:S(2)}) async-start(), calls=%async_computation.3 | async-start | bytes 2457600 | tf_op jit(solution)/shard_map/all_gather | solution.py:90
  8.0 5.0 collective-permute-start
  16.5 119.2 %all-gather.6.cloned.1.call-start = ((), (), s32[]{:S(2)}) async-start(), calls=%async_computation.4 | async-start | bytes 4915200 | tf_op jit(solution)/shard_map/all_gather | solution.py:122
  59.2 151.1 %all-gather.8.cloned.1.call-start = ((), (), s32[]{:S(2)}) async-start(), calls=%async_computation.5 | async-start | bytes 6635520 | tf_op jit(solution)/shard_map/all_gather | solution.py:101
  60.5 387.3 %reduce-scatter.10.cloned.1.call-start = ((), (), s32[]{:S(2)}) async-start(), calls=%async_computation.7 | async-start | bytes 4915200
  212.9 4.2 copy-start.7
  212.9 4.2 collective-permute-start.1
  215.7 4.5 slice-start
  217.1 3.0 slice-start.1
  233.4 4.0 collective-permute-start.2
  242.0 3.1 copy-start.5
  248.1 11.8 %collective-permute-start.3 = (f32[640,768]{1,0:T(8,128)}, f32[640,768]{1,0:T(8,128)}, u32[]{:S(2)}, u32[]{:S(2)}) collective-permute-start(f32[640,768]{1,0:T(8,128)} %fusion.64), channel_id=1, source_target_pairs={{0,1},{1,0},{2,3},{3,2},{4,5},{5,4},{6,7},{7,6},{8,9},{9,8},{10,11... | collective-permute-start | bytes 5898248 | tf_op jit(solution)/shard_map/ppermute | solution.py:34
  248.2 5.8 copy-start.6
  248.2 5.8 copy-start.21
  248.2 10.5 %collective-permute-start.4 = (bf16[1536]{0:T(1024)(128)(2,1)S(1)}, bf16[1536]{0:T(1024)(128)(2,1)S(1)}, u32[]{:S(2)}, u32[]{:S(2)}) collective-permute-start(bf16[1536]{0:T(1024)(128)(2,1)S(1)} %get-tuple-element.325), channel_id=1, source_target_pairs={{0,1},{1,0},{2,3},{3,2},{4,5},{5,4},{6,7},{7,6},{8,9},{9,8},{10,11... | collective-permute-start | bytes 9224 | tf_op jit(solution)/shard_map/ppermute | solution.py:40
  269.9 9.7 %copy-start.2 = (f32[640,768]{1,0:T(8,128)S(1)}, f32[640,768]{1,0:T(8,128)}, u32[]{:S(2)}) copy-start(f32[640,768]{1,0:T(8,128)} %copy-done.1) | copy-start | bytes 5898244
  376.4 73.3 %copy-start.16 = (bf16[640,768]{1,0:T(8,128)(2,1)S(1)}, bf16[640,768]{1,0:T(8,128)(2,1)}, u32[]{:S(2)}) copy-start(bf16[640,768]{1,0:T(8,128)(2,1)} %param.22) | copy-start | bytes 2949124
  376.4 120.4 %reduce-scatter.12.cloned.1.call-start = ((), (), s32[]{:S(2)}) async-start(), calls=%async_computation.8 | async-start | bytes 2457600
  377.7 1.2 collective-permute-start.6
  449.6 2.9 collective-permute-start.7
  462.1 101.2 %reduce-scatter.8.cloned.1.call-start = ((), (), s32[]{:S(2)}) async-start(), calls=%async_computation.6 | async-start | bytes 6881280 | tf_op jit(solution)/shard_map/reduce_scatter | solution.py:208
  462.6 186.3 %all-reduce.3.cloned.1.call-start = ((), (), s32[]{:S(2)}) async-start(), calls=%async_computation.9 | async-start | bytes 3940352 | tf_op jit(solution)/shard_map/psum | solution.py:261
  467.0 96.4 %copy-start.3 = (f32[640,768]{1,0:T(8,128)S(1)}, f32[640,768]{1,0:T(8,128)}, u32[]{:S(2)}) copy-start(f32[640,768]{1,0:T(8,128)} %copy-done.1) | copy-start | bytes 5898244
  467.0 96.3 %collective-permute-start.5 = (f32[640,768]{1,0:T(8,128)}, f32[640,768]{1,0:T(8,128)}, u32[]{:S(2)}, u32[]{:S(2)}) collective-permute-start(f32[640,768]{1,0:T(8,128)} %fusion.73), channel_id=1, source_target_pairs={{0,1},{1,0},{2,3},{3,2},{4,5},{5,4},{6,7},{7,6},{8,9},{9,8},{10,11... | collective-permute-start | bytes 5898248 | tf_op jit(solution)/shard_map/ppermute | solution.py:34
  (31 other events, 66.3 us)
Sparse Core Ops, SparseCore 0:
  16.6 36.4 all-gather.3
  59.3 76.3 all-gather.5
  137.6 60.3 all-gather.7
  376.5 71.2 reduce-scatter.9
  462.2 34.6 reduce-scatter.11
  499.8 63.4 reduce-scatter.7
  566.3 82.5 all-reduce.2

commit v3 on v2

--- a/solution.py
+++ b/solution.py
@@ -87,17 +87,15 @@
     shard_columns = jnp.stack(
         [output_bias, attn_gain, attn_shift, outer_bias, final_gain, final_shift], axis=1
     )
-    qkv_full = lax.all_gather(
-        jnp.concatenate(
-            [query_weight, key_weight, value_weight, shard_columns, bias_columns], axis=1
-        ),
+    kv_vec_full = lax.all_gather(
+        jnp.concatenate([key_weight, value_weight, shard_columns, bias_columns], axis=1),
         "shard", axis=0, tiled=True,
     )
-    vector_full = qkv_full[:, 3 * head_width :]
-    qkv_full = qkv_full[:, : 3 * head_width]
-    query_full = qkv_full[:, :head_width]
-    key_full = qkv_full[:, head_width : 2 * head_width]
-    value_full = qkv_full[:, 2 * head_width :]
+    query_full = lax.all_gather(query_weight, "shard", axis=0, tiled=True)
+    vector_full = kv_vec_full[:, 2 * head_width :]
+    key_full = kv_vec_full[:, :head_width]
+    value_full = kv_vec_full[:, head_width : 2 * head_width]
+    qkv_full = jnp.concatenate([query_full, kv_vec_full[:, : 2 * head_width]], axis=1)
     rest_full = lax.all_gather(
         jnp.concatenate([output_weight, inner_weight, outer_weight], axis=1),
         "shard", axis=0, tiled=True,
@@ -115,19 +113,28 @@
     value_shift = lax.dynamic_slice_in_dim(vbias_all, tensor_place * head_width, head_width).astype(f32)
     inner_shift = lax.dynamic_slice_in_dim(ibias_all, tensor_place * hidden_width, hidden_width).astype(f32)
 
-    projected = jnp.dot(tokens, qkv_full, preferred_element_type=f32)
-    query = (projected[:, :head_width] + query_shift).astype(jnp.bfloat16)
-    key_local = projected[:, head_width : 2 * head_width].astype(jnp.bfloat16)
-    value_local = (projected[:, 2 * head_width :] + value_shift).astype(jnp.bfloat16)
-    kv = lax.all_gather(
-        jnp.concatenate([key_local, value_local], axis=1), "ctx", axis=0, tiled=True
-    )
-    keys = kv[:, :head_width]
-    values = kv[:, head_width:]
+    projected = jnp.dot(tokens, kv_vec_full[:, : 2 * head_width], preferred_element_type=f32)
+    key_local = projected[:, :head_width].astype(jnp.bfloat16)
+    value_local = (projected[:, head_width:] + value_shift).astype(jnp.bfloat16)
+    query = (jnp.dot(tokens, query_full, preferred_element_type=f32) + query_shift).astype(
+        jnp.bfloat16
+    )
+    chunk_heads = 2 if head_count % 2 == 0 else 1
+    chunk_width = chunk_heads * HEAD_DIM
+    kv_chunks = []
+    for c in range(head_count // chunk_heads):
+        columns = slice(c * chunk_width, (c + 1) * chunk_width)
+        outgoing = jnp.concatenate([key_local[:, columns], value_local[:, columns]], axis=1)
+        kv_chunks.append(lax.all_gather(outgoing, "ctx", axis=0, tiled=True))
+    keys = jnp.concatenate([chunk[:, :chunk_width] for chunk in kv_chunks], axis=1)
+    values = jnp.concatenate([chunk[:, chunk_width:] for chunk in kv_chunks], axis=1)
     allowed = jnp.arange(keys.shape[0]) < seq_lengths[0]
 
+    def split_heads_of(matrix, count):
+        return matrix.reshape(matrix.shape[0], count, HEAD_DIM).transpose(1, 0, 2)
+
     def split_heads(matrix):
-        return matrix.reshape(matrix.shape[0], head_count, HEAD_DIM).transpose(1, 0, 2)
+        return split_heads_of(matrix, head_count)
 
     def join_heads(stacked):
         return stacked.transpose(1, 0, 2).reshape(stacked.shape[1], head_width)
@@ -152,7 +159,21 @@
     query_heads = split_heads(query)
     key_heads = split_heads(keys)
     value_heads = split_heads(values)
-    context_heads, log_sums = lax.map(head_forward, (query_heads, key_heads, value_heads))
+    chunk_outs = []
+    for c, chunk in enumerate(kv_chunks):
+        heads = slice(c * chunk_heads, (c + 1) * chunk_heads)
+        chunk_outs.append(
+            lax.map(
+                head_forward,
+                (
+                    query_heads[heads],
+                    split_heads_of(chunk[:, :chunk_width], chunk_heads),
+                    split_heads_of(chunk[:, chunk_width:], chunk_heads),
+                ),
+            )
+        )
+    context_heads = jnp.concatenate([o[0] for o in chunk_outs])
+    log_sums = jnp.concatenate([o[1] for o in chunk_outs])
     context = join_heads(context_heads)
     attn_part = jnp.einsum("th,oh->to", context, output_full, preferred_element_type=f32)
     attended = tp_sum(attn_part) + outbias_full
@@ -203,21 +224,8 @@
         ],
         axis=1,
     ).astype(low)
-    early, dcontext = lax.optimization_barrier((early, dcontext))
-    early_piece = lax.psum(
-        lax.psum_scatter(early, "shard", scatter_dimension=0, tiled=True), "ctx"
-    ).astype(f32)
-    output_total = early_piece[:, :head_width]
-    inner_total = early_piece[:, head_width : head_width + hidden_width]
-    outer_total = early_piece[:, head_width + hidden_width : head_width + 2 * hidden_width]
-    early_vectors = early_piece[:, head_width + 2 * hidden_width :]
-    outbias_total, attn_gain_total, attn_shift_total, outerbias_total, final_gain_total, final_shift_total = (
-        early_vectors[:, :6].T
-    )
+    early_scattered = lax.psum_scatter(early, "shard", scatter_dimension=0, tiled=True)
     local_rows = piece // tensor_count
-    ibias_total = lax.dynamic_slice_in_dim(
-        early_vectors[:, 6:], tensor_place * local_rows, local_rows, 0
-    ).reshape(-1)
 
     def head_backward(quintet):
         query_head, key_head, value_head, dcontext_head, log_sum = quintet
@@ -238,10 +246,24 @@
         head_backward, (query_heads, key_heads, value_heads, split_heads(dcontext), log_sums)
     )
     dquery = join_heads(dquery_heads)
-    dkv = lax.psum_scatter(
-        jnp.concatenate([join_heads(dkey_heads), join_heads(dvalue_heads)], axis=1).astype(low),
-        "ctx", scatter_dimension=0, tiled=True,
-    ).astype(jnp.bfloat16)
+    dkv_partial = jnp.concatenate(
+        [join_heads(dkey_heads), join_heads(dvalue_heads)], axis=1
+    ).astype(low)
+    dkv_partial, early_scattered = lax.optimization_barrier((dkv_partial, early_scattered))
+    dkv = lax.psum_scatter(dkv_partial, "ctx", scatter_dimension=0, tiled=True).astype(
+        jnp.bfloat16
+    )
+    early_piece = lax.psum(early_scattered, "ctx").astype(f32)
+    output_total = early_piece[:, :head_width]
+    inner_total = early_piece[:, head_width : head_width + hidden_width]
+    outer_total = early_piece[:, head_width + hidden_width : head_width + 2 * hidden_width]
+    early_vectors = early_piece[:, head_width + 2 * hidden_width :]
+    outbias_total, attn_gain_total, attn_shift_total, outerbias_total, final_gain_total, final_shift_total = (
+        early_vectors[:, :6].T
+    )
+    ibias_total = lax.dynamic_slice_in_dim(
+        early_vectors[:, 6:], tensor_place * local_rows, local_rows, 0
+    ).reshape(-1)
     dkeys = dkv[:, :head_width]
     dvalues = dkv[:, head_width:]
     dqkv = jnp.concatenate([dquery, dkeys, dvalues], axis=1)

time: 675 us -> 633 us (0.938)
  waiting for transfers between devices: 362 us -> 288 us
  local copies, waits for them, and re-layouts: 82 us -> 98.5 us
  blocking collectives: 0 us -> 10.6 us
  other arithmetic: 47.1 us -> 56.9 us
    reduce_scatter x1, waiting for transfers between devices: 64.3 us -> 0.01 us  [on_device(): lax.psum_scatter(early, 'shard', scatter_dimension=0, tiled=True)]
    all_gather x2 -> x4, waiting for transfers between devices: 111 us -> 89.2 us  [the longest x3 57.5 us: on_device(): kv_chunks.append(lax.all_gather(outgoing, 'ctx', axis=0, tiled=True))]
    all_gather x1, waiting for transfers between devices: 0.02 us -> 12.7 us  [on_device(): lax.all_gather(jnp.concatenate([output_weight, inner_weight, outer_weight...]
    reshape x3 -> x10, local copies, waits for them, and re-layouts: 8.41 us -> 19.5 us  [split_heads_of(): return matrix.reshape(matrix.shape[0], count, HEAD_DIM).transpose(1, 0, 2)]
    all_gather x0 -> x1, blocking collectives: none -> 10.6 us  [on_device(): query_full = lax.all_gather(query_weight, 'shard', axis=0, tiled=True)]
    concatenate x1 -> x7, other arithmetic: 1.03 us -> 8.71 us  [the longest x1 2.5 us: on_device(): jnp.concatenate([chunk[:, chunk_width:] for chunk in kv_chunks], axis=1)]
    unnamed x9 -> x11, waiting for transfers between devices: 99 us -> 100 us
    unnamed x53 -> x101, local copies, waits for them, and re-layouts: 20.1 us -> 21.3 us
  transfers between devices with their start and end apart: 15 -> 17, of which waited for: 9 -> 11; matrix products, arithmetic and copies ran while one was open for 15% -> 34% of each run, Pallas kernels for 0% -> 0%
where the time goes in v3:
time: 633 us; the launch traced here: 628 us
  waiting for transfers between devices  288 us (45%)
  matrix products  155 us (24%)
  local copies, waits for them, and re-layouts  98.5 us (16%)
  other arithmetic  56.9 us (9%)
  between operations  15.1 us (2%)
  blocking collectives  10.6 us (2%)
    unnamed x11, waiting for transfers between devices  100 us
    psum x1, waiting for transfers between devices, on_device(): lax.psum(lax.psum_scatter(late, 'shard', scatter_dimension=0, tiled=True)...  79.8 us
    all_gather x3, waiting for transfers between devices, on_device(): kv_chunks.append(lax.all_gather(outgoing, 'ctx', axis=0, tiled=True))  57.5 us
    all_gather x1, waiting for transfers between devices, on_device(): lax.all_gather(jnp.concatenate([key_weight, value_weight, shard_columns,...  31.7 us
    dot_general x12, matrix products, scores_of(): jnp.einsum('qd,kd->qk', query_head, key_head, preferred_element_type=f32)  30.3 us
    dot_general x6, matrix products, head_forward(): mixed = jnp.dot(portion, value_head, preferred_element_type=f32)  27.8 us
    unnamed x101, local copies, waits for them, and re-layouts  21.3 us
    reshape x10, local copies, waits for them, and re-layouts, split_heads_of(): return matrix.reshape(matrix.shape[0], count, HEAD_DIM).transpose(1, 0, 2)  19.5 us
  transfers between devices with their start and end apart: 17, of which 11 were waited for; matrix products, arithmetic and copies ran while one was open for 34% of the time, Pallas kernels for 0%

profile of v3, /device:TPU:0, one launch (start us, length us, event | category | flops | bytes accessed | tf_op | source)
XLA Modules:
  0.0 627.5 jit_solution(12758260347536476679)
XLA Ops:
  16.6 31.7 %all-gather.6.cloned.1.call-done = bf16[768,780]{1,0:T(8,128)(2,1)} async-done(((bf16[192,780]{1,0:T(8,128)(2,1)}), bf16[768,780]{1,0:T(8,128)(2,1)}) %all-gather.6.cloned.1.call-update) | async-done | bytes 1198096 | tf_op jit(solution)/shard_map/all_gather | solution.py:90
  56.0 10.6 %all_gather.18 = bf16[768,384]{1,0:T(8,128)(2,1)S(1)} all-gather(bf16[192,384]{1,0:T(8,128)(2,1)S(1)} %copy-done.38), channel_id=1, replica_groups=mesh['shard'=4,'ctx'=4,'tp'=2] {'shard'}, dimensions={0}, use_global_device_ids=true | all-gather | bytes 737280 | tf_op jit(solution)/shard_map/all_gather | solution.py:94
  69.0 16.6 %all-gather.8.cloned.1.call-done = bf16[2560,256]{0,1:T(8,128)(2,1)} async-done(((bf16[640,256]{0,1:T(8,128)(2,1)}), bf16[2560,256]{0,1:T(8,128)(2,1)}) %all-gather.8.cloned.1.call-update) | async-done | bytes 1310736 | tf_op jit(solution)/shard_map/all_gather | solution.py:128
  89.2 18.7 %while.54 = (s32[]{:T(128)}, bf16[2,640,64]{1,2,0:T(8,128)(2,1)S(1)}, f32[2,640]{1,0:T(2,128)S(1)}, bf16[2,640,64]{2,1,0:T(8,128)(2,1)S(1)}, bf16[2,2560,64]{2,1...) while((s32[]{:T(128)}, ...), condition=%wide.region_3.4_spmd.clone, body=%wide.region_0.3_spmd.clone.sunk | while | flops 439134080 | bytes 50100380 | solution.py:166
  93.9 4.7 fusion.185
  103.2 4.6 fusion.185
  107.9 10.9 %all-gather.10.cloned.1.call-done = bf16[2560,256]{0,1:T(8,128)(2,1)} async-done(((bf16[640,256]{0,1:T(8,128)(2,1)}), bf16[2560,256]{0,1:T(8,128)(2,1)}) %all-gather.10.cloned.1.call-update) | async-done | bytes 1310736 | tf_op jit(solution)/shard_map/all_gather | solution.py:128
  122.4 30.0 %all-gather.12.cloned.1.call-done = bf16[2560,256]{0,1:T(8,128)(2,1)} async-done(((bf16[640,256]{0,1:T(8,128)(2,1)}), bf16[2560,256]{0,1:T(8,128)(2,1)}) %all-gather.12.cloned.1.call-update) | async-done | bytes 1310736 | tf_op jit(solution)/shard_map/all_gather | solution.py:128
  158.0 20.9 %while.55 = (s32[]{:T(128)}, bf16[2,640,64]{1,2,0:T(8,128)(2,1)S(1)}, f32[2,640]{1,0:T(2,128)S(1)}, bf16[2,640,64]{2,1,0:T(8,128)(2,1)}, bf16[2,2560,64]{2,1,0:T...) while((s32[]{:T(128)}, ...), condition=%wide.region_7.8_spmd.clone, body=%wide.region_4.7_spmd.clone.sunk | while | flops 439134080 | bytes 47478912 | solution.py:166
  164.0 4.7 fusion.189
  174.2 4.7 fusion.189
  179.6 21.6 %while.56 = (s32[]{:T(128)}, bf16[2,640,64]{1,2,0:T(8,128)(2,1)S(1)}, f32[2,640]{1,0:T(2,128)S(1)}, bf16[2,640,64]{2,1,0:T(8,128)(2,1)}, bf16[2,2560,64]{2,1,0:T...) while((s32[]{:T(128)}, ...), condition=%wide.region_11.12_spmd.clone, body=%wide.region_8.11_spmd.clone.sunk | while | flops 439134080 | bytes 50100380 | solution.py:166
  203.2 12.7 %all-gather.14.cloned.1.call-done = bf16[768,3456]{1,0:T(8,128)(2,1)} async-done(((bf16[192,3456]{1,0:T(8,128)(2,1)}), bf16[768,3456]{1,0:T(8,128)(2,1)}) %all-gather.14.cloned.1.call-update) | async-done | bytes 5308432 | tf_op jit(solution)/shard_map/all_gather | solution.py:99
  225.1 12.0 %multiply_convert_fusion.1 = (bf16[640,1536]{1,0:T(8,128)(2,1)S(1)}, f32[640,1536]{1,0:T(8,128)}, f32[640,1536]{1,0:T(8,128)}) fusion(f32[1536]{0:T(1024)S(1)} %dynamic-slice_convert_fusion, bf16[768,3456]{1,0:T(8,128)(2,1)S(1)} %bitcast.230, f32[640,768]{1,0:T(8,128)S(1)} %get-tuple-element.416, f32[768]{0:T(1024)S(1)} %get-tuple-element.333, ...), kind=kOutput, calls=%fused_computation.110 | convolution fusion | flops 1577287680 | bytes 14180352 | tf_op jit(solution)/shard_map/dot_general | solution.py:183
  260.0 4.9 copy.92
  267.4 4.9 copy.94
  273.3 5.4 convolution_convert_fusion.2
  293.1 8.9 %concatenate.60 = bf16[768,3466]{1,0:T(8,128)(2,1)} concatenate(bf16[768,384]{1,0:T(8,128)(2,1)S(1)} %copy.95, bf16[768,1536]{1,0:T(8,128)(2,1)S(1)} %copy-done.27, bf16[768,1536]{1,0:T(8,128)(2,1)} %convolution_convert_fusion.1, bf16[768,1]{1,0:T(8,128)(2,1)S(1)} %stack.117, bf16[768,1]{1,0:T(8,128)(2,1)S(1)} %stack.118, bf16[768,1]{1,0:T(8,128)(2,1)S(1)} %stack.119, ...), dimensions={1} | concatenate | bytes 10647552 | tf_op jit(solution)/shard_map/concatenate | solution.py:213
  307.7 85.3 %while.57 = (s32[]{:T(128)}, bf16[6,640,64]{1,2,0:T(8,128)(2,1)}, bf16[6,2560,64]{1,2,0:T(8,128)(2,1)}, bf16[6,2560,64]{1,2,0:T(8,128)(2,1)}, bf16[6,640,64]{2,1...) while((s32[]{:T(128)}, bf16[6,640,64]{1,2,0:T(8,128)(2,1)}, ...), condition=%wide.region_22.23_spmd.clone, body=%wide.region_20.22_spmd.clone.sunk | while | flops 1063569280 | bytes 53189236 | solution.py:245
  397.3 6.3 copy.105
  406.1 70.0 %reduce-scatter.10.cloned.1.call-done = bf16[640,768]{1,0:T(8,128)(2,1)} async-done(((bf16[2560,768]{1,0:T(8,128)(2,1)}), bf16[640,768]{1,0:T(8,128)(2,1)}) %reduce-scatter.10.cloned.1.call-update) | async-done | bytes 983056
  480.7 7.2 %concatenate.63 = bf16[768,1154]{0,1:T(8,128)(2,1)S(1)} concatenate(bf16[768,1152]{0,1:T(8,128)(2,1)} %fusion.92, bf16[768,1]{0,1:T(2,128)(2,1)S(1)} %bitcast.233, bf16[768,1]{0,1:T(2,128)(2,1)S(1)} %bitcast.234), dimensions={1} | concatenate | bytes 3545088 | tf_op jit(solution)/shard_map/concatenate | solution.py:275
  495.0 30.1 %reduce-scatter.12.cloned.1.call-done = bf16[192,1154]{1,0:T(8,128)(2,1)} async-done(((bf16[768,1154]{1,0:T(8,128)(2,1)}), bf16[192,1154]{1,0:T(8,128)(2,1)}) %reduce-scatter.12.cloned.1.call-update) | async-done | bytes 443152
  531.0 79.8 %all-reduce.3.cloned.1.call-done = (bf16[192,1154]{0,1:T(8,128)(2,1)}, bf16[192,3466]{1,0:T(8,128)(2,1)}) async-done(((bf16[192,1154]{0,1:T(8,128)(2,1)}, bf16[192,3466]{1,0:T(8,128)(2,1)}), (bf16[192,1154]{0,1:T(8,128)(2,1)}, bf16[192,3466]{1,0:T(8,128)(2,1)})) %all-reduce.3.cloned.1.call-update) | async-done | bytes 1774096 | tf_op jit(solution)/shard_map/psum | solution.py:283
  (364 shorter events, 250.5 us)
Async XLA Ops:
  7.2 42.4 %copy-start.24 = (bf16[640,768]{1,0:T(8,128)(2,1)S(1)}, bf16[640,768]{1,0:T(8,128)(2,1)}, u32[]{:S(2)}) copy-start(bf16[640,768]{1,0:T(8,128)(2,1)} %param.26) | copy-start | bytes 2949124
  7.2 41.1 %all-gather.6.cloned.1.call-start = ((), (), s32[]{:S(2)}) async-start(), calls=%async_computation.3 | async-start | bytes 1720320 | tf_op jit(solution)/shard_map/all_gather | solution.py:90
  8.1 5.0 collective-permute-start
  16.5 69.0 %all-gather.8.cloned.1.call-start = ((), (), s32[]{:S(2)}) async-start(), calls=%async_computation.4 | async-start | bytes 1638400 | tf_op jit(solution)/shard_map/all_gather | solution.py:128
  53.0 65.7 %all-gather.10.cloned.1.call-start = ((), (), s32[]{:S(2)}) async-start(), calls=%async_computation.5 | async-start | bytes 1638400 | tf_op jit(solution)/shard_map/all_gather | solution.py:128
  53.9 98.6 %all-gather.12.cloned.1.call-start = ((), (), s32[]{:S(2)}) async-start(), calls=%async_computation.6 | async-start | bytes 1638400 | tf_op jit(solution)/shard_map/all_gather | solution.py:128
  54.7 161.2 %all-gather.14.cloned.1.call-start = ((), (), s32[]{:S(2)}) async-start(), calls=%async_computation.7 | async-start | bytes 6635520 | tf_op jit(solution)/shard_map/all_gather | solution.py:99
  56.0 341.3 %reduce-scatter.8.cloned.1.call-start = ((), (), s32[]{:S(2)}) async-start(), calls=%async_computation.8 | async-start | bytes 6881280 | tf_op jit(solution)/shard_map/reduce_scatter | solution.py:227
  68.0 18.9 %copy-start.6 = (bf16[640,6,64]{2,0,1:T(8,128)(2,1)}, bf16[640,6,64]{2,0,1:T(8,128)(2,1)S(1)}, u32[]{:S(2)}) copy-start(bf16[640,6,64]{2,0,1:T(8,128)(2,1)S(1)} %copy.85) | copy-start | bytes 1474564
  120.1 34.5 %copy-start.16 = (bf16[2560,128]{0,1:T(8,128)(2,1)}, bf16[2560,128]{0,1:T(8,128)(2,1)S(1)}, u32[]{:S(2)}) copy-start(bf16[2560,128]{0,1:T(8,128)(2,1)S(1)} %get-tuple-element.432) | copy-start | bytes 1966084
  120.2 34.5 %copy-start.18 = (bf16[2560,128]{0,1:T(8,128)(2,1)}, bf16[2560,128]{0,1:T(8,128)(2,1)S(1)}, u32[]{:S(2)}) copy-start(bf16[2560,128]{0,1:T(8,128)(2,1)S(1)} %get-tuple-element.433) | copy-start | bytes 1966084
  201.3 16.6 %copy-start.11 = (bf16[768,780]{1,0:T(8,128)(2,1)S(1)}, bf16[768,780]{1,0:T(8,128)(2,1)}, u32[]{:S(2)}) copy-start(bf16[768,780]{1,0:T(8,128)(2,1)} %all-gather.6.cloned.1.call-done) | copy-start | bytes 3594244
  217.8 4.2 collective-permute-start.1
  240.1 4.3 collective-permute-start.2
  258.5 27.4 %collective-permute-start.3 = (f32[640,768]{1,0:T(8,128)}, f32[640,768]{1,0:T(8,128)}, u32[]{:S(2)}, u32[]{:S(2)}) collective-permute-start(f32[640,768]{1,0:T(8,128)} %fusion.102), channel_id=1, source_target_pairs={{0,1},{1,0},{2,3},{3,2},{4,5},{5,4},{6,7},{7,6},{8,9},{9,8},{10,11... | collective-permute-start | bytes 5898248 | tf_op jit(solution)/shard_map/ppermute | solution.py:34
  272.9 11.8 %collective-permute-start.4 = (bf16[1536]{0:T(1024)(128)(2,1)S(1)}, bf16[1536]{0:T(1024)(128)(2,1)S(1)}, u32[]{:S(2)}, u32[]{:S(2)}) collective-permute-start(bf16[1536]{0:T(1024)(128)(2,1)S(1)} %get-tuple-element.464), channel_id=1, source_target_pairs={{0,1},{1,0},{2,3},{3,2},{4,5},{5,4},{6,7},{7,6},{8,9},{9,8},{10,11... | collective-permute-start | bytes 9224 | tf_op jit(solution)/shard_map/ppermute | solution.py:40
  302.1 174.0 %reduce-scatter.10.cloned.1.call-start = ((), (), s32[]{:S(2)}) async-start(), calls=%async_computation.9 | async-start | bytes 4915200
  403.6 74.3 %copy-start.26 = (bf16[640,768]{1,0:T(8,128)(2,1)S(1)}, bf16[640,768]{1,0:T(8,128)(2,1)}, u32[]{:S(2)}) copy-start(bf16[640,768]{1,0:T(8,128)(2,1)} %param.26) | copy-start | bytes 2949124
  403.6 121.5 %reduce-scatter.12.cloned.1.call-start = ((), (), s32[]{:S(2)}) async-start(), calls=%async_computation.10 | async-start | bytes 2457600
  404.8 1.2 collective-permute-start.6
  477.8 2.9 collective-permute-start.7
  490.3 120.5 %all-reduce.3.cloned.1.call-start = ((), (), s32[]{:S(2)}) async-start(), calls=%async_computation.11 | async-start | bytes 3940352 | tf_op jit(solution)/shard_map/psum | solution.py:283
  494.5 32.8 %copy-start.5 = (f32[640,768]{1,0:T(8,128)S(1)}, f32[640,768]{1,0:T(8,128)}, u32[]{:S(2)}) copy-start(f32[640,768]{1,0:T(8,128)} %copy-done.3) | copy-start | bytes 5898244
  494.5 32.7 %collective-permute-start.5 = (f32[640,768]{1,0:T(8,128)}, f32[640,768]{1,0:T(8,128)}, u32[]{:S(2)}, u32[]{:S(2)}) collective-permute-start(f32[640,768]{1,0:T(8,128)} %fusion.110), channel_id=1, source_target_pairs={{0,1},{1,0},{2,3},{3,2},{4,5},{5,4},{6,7},{7,6},{8,9},{9,8},{10,11... | collective-permute-start | bytes 5898248 | tf_op jit(solution)/shard_map/ppermute | solution.py:34
  (50 other events, 174.9 us)
Sparse Core Ops, SparseCore 0:
  16.6 31.5 all-gather.5
  53.2 32.2 all-gather.7
  87.1 31.6 all-gather.9
  120.8 31.6 all-gather.11
  154.7 61.1 all-gather.13
  302.2 63.4 reduce-scatter.7
  403.7 72.3 reduce-scatter.9
  490.4 34.6 reduce-scatter.11
  528.1 82.5 all-reduce.2

commit v4 on v3

--- a/solution.py
+++ b/solution.py
@@ -1,9 +1,128 @@
+import functools
+
 import jax
 import jax.numpy as jnp
 from jax import lax
+from jax.experimental import pallas as pl
+from jax.experimental.pallas import tpu as pltpu
 from jax.sharding import PartitionSpec as P
 
 HEAD_DIM = 64
+QUERY_TILE = 128
+
+
+def _scores(length_ref, q, k, factor):
+    s = lax.dot_general(q, k, (((1,), (1,)), ((), ())), preferred_element_type=jnp.float32) * factor
+    keys = lax.broadcasted_iota(jnp.int32, s.shape, 1)
+    return jnp.where(keys < length_ref[0], s, -1e30)
+
+
+def _attend_kernel(length_ref, q_ref, kv_ref, o_ref, lse_ref, *, heads, factor):
+    for h in range(heads):
+        cols = slice(h * HEAD_DIM, (h + 1) * HEAD_DIM)
+        vcols = slice((heads + h) * HEAD_DIM, (heads + h + 1) * HEAD_DIM)
+        s = _scores(length_ref, q_ref[:, cols], kv_ref[:, cols], factor)
+        highest = jnp.max(s, axis=1, keepdims=True)
+        shifted = jnp.exp(s - highest)
+        summed = jnp.sum(shifted, axis=1, keepdims=True)
+        portion = (shifted / summed).astype(jnp.bfloat16)
+        mixed = jnp.dot(portion, kv_ref[:, vcols], preferred_element_type=jnp.float32)
+        o_ref[:, cols] = mixed.astype(o_ref.dtype)
+        lse_ref[:, h : h + 1] = highest + jnp.log(summed)
+
+
+def attend(length, q, kv, factor):
+    n, width = q.shape
+    m = kv.shape[0]
+    heads = width // HEAD_DIM
+    tq = min(QUERY_TILE, n)
+    grid = pltpu.PrefetchScalarGridSpec(
+        num_scalar_prefetch=1,
+        grid=(n // tq,),
+        in_specs=[
+            pl.BlockSpec((tq, width), lambda i, length: (i, 0)),
+            pl.BlockSpec((m, 2 * width), lambda i, length: (0, 0)),
+        ],
+        out_specs=[
+            pl.BlockSpec((tq, width), lambda i, length: (i, 0)),
+            pl.BlockSpec((tq, heads), lambda i, length: (i, 0)),
+        ],
+    )
+    flops = 4 * n * m * width
+    return pl.pallas_call(
+        functools.partial(_attend_kernel, heads=heads, factor=factor),
+        grid_spec=grid,
+        out_shape=(
+            jax.ShapeDtypeStruct((n, width), jnp.bfloat16),
+            jax.ShapeDtypeStruct((n, heads), jnp.float32),
+        ),
+        compiler_params=pltpu.CompilerParams(dimension_semantics=("arbitrary",)),
+        cost_estimate=pl.CostEstimate(
+            flops=flops, transcendentals=n * m * heads, bytes_accessed=2 * (2 * n * width + 2 * m * width)
+        ),
+    )(length, q, kv)
+
+
+def _attend_back_kernel(length_ref, q_ref, kv_ref, do_ref, lse_ref, dq_ref, dkv_ref, *, heads, factor):
+    @pl.when(pl.program_id(0) == 0)
+    def _():
+        dkv_ref[...] = jnp.zeros_like(dkv_ref)
+
+    for h in range(heads):
+        cols = slice(h * HEAD_DIM, (h + 1) * HEAD_DIM)
+        vcols = slice((heads + h) * HEAD_DIM, (heads + h + 1) * HEAD_DIM)
+        q = q_ref[:, cols]
+        k = kv_ref[:, cols]
+        v = kv_ref[:, vcols]
+        do = do_ref[:, cols]
+        portion = jnp.exp(_scores(length_ref, q, k, factor) - lse_ref[:, h : h + 1])
+        dportion = lax.dot_general(do, v, (((1,), (1,)), ((), ())), preferred_element_type=jnp.float32)
+        dkv_ref[:, vcols] += lax.dot_general(
+            portion.astype(jnp.bfloat16), do, (((0,), (0,)), ((), ())), preferred_element_type=jnp.float32
+        )
+        centering = jnp.sum(portion * dportion, axis=1, keepdims=True)
+        dscores = (portion * (dportion - centering)).astype(jnp.bfloat16)
+        dq_ref[:, cols] = (
+            jnp.dot(dscores, k, preferred_element_type=jnp.float32) * factor
+        ).astype(dq_ref.dtype)
+        dkv_ref[:, cols] += (
+            lax.dot_general(dscores, q, (((0,), (0,)), ((), ())), preferred_element_type=jnp.float32) * factor
+        )
+
+
+def attend_back(length, q, kv, do, lse, factor):
+    n, width = q.shape
+    m = kv.shape[0]
+    heads = width // HEAD_DIM
+    tq = min(QUERY_TILE, n)
+    grid = pltpu.PrefetchScalarGridSpec(
+        num_scalar_prefetch=1,
+        grid=(n // tq,),
+        in_specs=[
+            pl.BlockSpec((tq, width), lambda i, length: (i, 0)),
+            pl.BlockSpec((m, 2 * width), lambda i, length: (0, 0)),
+            pl.BlockSpec((tq, width), lambda i, length: (i, 0)),
+            pl.BlockSpec((tq, heads), lambda i, length: (i, 0)),
+        ],
+        out_specs=[
+            pl.BlockSpec((tq, width), lambda i, length: (i, 0)),
+            pl.BlockSpec((m, 2 * width), lambda i, length: (0, 0)),
+        ],
+    )
+    flops = 10 * n * m * width
+    return pl.pallas_call(
+        functools.partial(_attend_back_kernel, heads=heads, factor=factor),
+        grid_spec=grid,
+        out_shape=(
+            jax.ShapeDtypeStruct((n, width), jnp.bfloat16),
+            jax.ShapeDtypeStruct((m, 2 * width), jnp.float32),
+        ),
+        compiler_params=pltpu.CompilerParams(dimension_semantics=("arbitrary",)),
+        cost_estimate=pl.CostEstimate(
+            flops=flops, transcendentals=n * m * heads,
+            bytes_accessed=2 * (3 * n * width + 2 * m * width) + 4 * 2 * m * width,
+        ),
+    )(length, q, kv, do, lse)
 
 
 EPSILON = 1e-12
@@ -126,55 +245,11 @@
         columns = slice(c * chunk_width, (c + 1) * chunk_width)
         outgoing = jnp.concatenate([key_local[:, columns], value_local[:, columns]], axis=1)
         kv_chunks.append(lax.all_gather(outgoing, "ctx", axis=0, tiled=True))
-    keys = jnp.concatenate([chunk[:, :chunk_width] for chunk in kv_chunks], axis=1)
-    values = jnp.concatenate([chunk[:, chunk_width:] for chunk in kv_chunks], axis=1)
-    allowed = jnp.arange(keys.shape[0]) < seq_lengths[0]
-
-    def split_heads_of(matrix, count):
-        return matrix.reshape(matrix.shape[0], count, HEAD_DIM).transpose(1, 0, 2)
-
-    def split_heads(matrix):
-        return split_heads_of(matrix, head_count)
-
-    def join_heads(stacked):
-        return stacked.transpose(1, 0, 2).reshape(stacked.shape[1], head_width)
-
-    def scores_of(query_head, key_head):
-        scores = (
-            jnp.einsum("qd,kd->qk", query_head, key_head, preferred_element_type=f32)
-            * factor
-        )
-        return jnp.where(allowed[None, :], scores, -1e30)
-
-    def head_forward(triple):
-        query_head, key_head, value_head = triple
-        scores = scores_of(query_head, key_head)
-        highest = jnp.max(scores, -1, keepdims=True)
-        shifted = jnp.exp(scores - highest)
-        summed = jnp.sum(shifted, -1, keepdims=True)
-        portion = (shifted / summed).astype(jnp.bfloat16)
-        mixed = jnp.dot(portion, value_head, preferred_element_type=f32)
-        return (mixed.astype(jnp.bfloat16), (highest + jnp.log(summed))[:, 0])
-
-    query_heads = split_heads(query)
-    key_heads = split_heads(keys)
-    value_heads = split_heads(values)
-    chunk_outs = []
-    for c, chunk in enumerate(kv_chunks):
-        heads = slice(c * chunk_heads, (c + 1) * chunk_heads)
-        chunk_outs.append(
-            lax.map(
-                head_forward,
-                (
-                    query_heads[heads],
-                    split_heads_of(chunk[:, :chunk_width], chunk_heads),
-                    split_heads_of(chunk[:, chunk_width:], chunk_heads),
-                ),
-            )
-        )
-    context_heads = jnp.concatenate([o[0] for o in chunk_outs])
-    log_sums = jnp.concatenate([o[1] for o in chunk_outs])
-    context = join_heads(context_heads)
+    chunk_outs = [
+        attend(seq_lengths, query[:, c * chunk_width : (c + 1) * chunk_width], chunk, factor)
+        for c, chunk in enumerate(kv_chunks)
+    ]
+    context = jnp.concatenate([o[0] for o in chunk_outs], axis=1)
     attn_part = jnp.einsum("th,oh->to", context, output_full, preferred_element_type=f32)
     attended = tp_sum(attn_part) + outbias_full
     normal_first, inverse_first = norm_parts(tokens.astype(f32) + attended)
@@ -227,28 +302,19 @@
     early_scattered = lax.psum_scatter(early, "shard", scatter_dimension=0, tiled=True)
     local_rows = piece // tensor_count
 
-    def head_backward(quintet):
-        query_head, key_head, value_head, dcontext_head, log_sum = quintet
-        portion = jnp.exp(scores_of(query_head, key_head) - log_sum[:, None])
-        dportion = jnp.einsum("qd,kd->qk", dcontext_head, value_head, preferred_element_type=f32)
-        dvalue_head = jnp.einsum(
-            "qk,qd->kd", portion.astype(jnp.bfloat16), dcontext_head, preferred_element_type=f32
+    chunk_backs = [
+        attend_back(
+            seq_lengths,
+            query[:, c * chunk_width : (c + 1) * chunk_width],
+            chunk,
+            dcontext[:, c * chunk_width : (c + 1) * chunk_width],
+            chunk_outs[c][1],
+            factor,
         )
-        centering = jnp.sum(portion * dportion, -1, keepdims=True)
-        dscores = (portion * (dportion - centering)).astype(jnp.bfloat16)
-        dquery_head = jnp.dot(dscores, key_head, preferred_element_type=f32) * factor
-        dkey_head = (
-            jnp.einsum("qk,qd->kd", dscores, query_head, preferred_element_type=f32) * factor
-        )
-        return (dquery_head.astype(jnp.bfloat16), dkey_head, dvalue_head)
-
-    dquery_heads, dkey_heads, dvalue_heads = lax.map(
-        head_backward, (query_heads, key_heads, value_heads, split_heads(dcontext), log_sums)
-    )
-    dquery = join_heads(dquery_heads)
-    dkv_partial = jnp.concatenate(
-        [join_heads(dkey_heads), join_heads(dvalue_heads)], axis=1
-    ).astype(low)
+        for c, chunk in enumerate(kv_chunks)
+    ]
+    dquery = jnp.concatenate([back[0] for back in chunk_backs], axis=1)
+    dkv_partial = jnp.concatenate([back[1] for back in chunk_backs], axis=1).astype(low)
     dkv_partial, early_scattered = lax.optimization_barrier((dkv_partial, early_scattered))
     dkv = lax.psum_scatter(dkv_partial, "ctx", scatter_dimension=0, tiled=True).astype(
         jnp.bfloat16
@@ -264,8 +330,14 @@
     ibias_total = lax.dynamic_slice_in_dim(
         early_vectors[:, 6:], tensor_place * local_rows, local_rows, 0
     ).reshape(-1)
-    dkeys = dkv[:, :head_width]
-    dvalues = dkv[:, head_width:]
+    dkeys = jnp.concatenate(
+        [dkv[:, 2 * c * chunk_width : (2 * c + 1) * chunk_width] for c in range(len(kv_chunks))],
+        axis=1,
+    )
+    dvalues = jnp.concatenate(
+        [dkv[:, (2 * c + 1) * chunk_width : (2 * c + 2) * chunk_width] for c in range(len(kv_chunks))],
+        axis=1,
+    )
     dqkv = jnp.concatenate([dquery, dkeys, dvalues], axis=1)
     qkv_weight_part = jnp.einsum("td,th->dh", tokens, dqkv, preferred_element_type=f32)
     query_bias_part = jnp.sum(dquery.astype(f32), 0)

time: 633 us -> 604 us (0.954)
  matrix products: 155 us -> 41.8 us
  Pallas kernels: 0 us -> 89.5 us
  waiting for transfers between devices: 288 us -> 322 us
  other arithmetic: 56.9 us -> 35.5 us
  local copies, waits for them, and re-layouts: 98.5 us -> 78.7 us
    dot_general x42 -> x0, matrix products: 111 us -> none  [the longest x12 30.3 us: scores_of(): jnp.einsum('qd,kd->qk', query_head, key_head, preferred_element_type=f32)]
    pallas_call x0 -> x6, Pallas kernels: none -> 89.5 us  [the longest x3 55.8 us: attend_back(): pl.pallas_call(functools.partial(_attend_back_kernel, heads=heads, factor...]
    unnamed x11 -> x10, waiting for transfers between devices: 100 us -> 28.9 us
    reduce_scatter x0 -> x1, waiting for transfers between devices: none -> 66.3 us  [on_device(): lax.psum_scatter(dkv_partial, 'ctx', scatter_dimension=0, tiled=True)]
    all_gather x1, waiting for transfers between devices: 12.7 us -> 48.9 us  [on_device(): lax.all_gather(jnp.concatenate([output_weight, inner_weight, outer_weight...]
    reshape x10 -> x0, local copies, waits for them, and re-layouts: 19.5 us -> none  [split_heads_of(): return matrix.reshape(matrix.shape[0], count, HEAD_DIM).transpose(1, 0, 2)]
    while x20 -> x0, local copies, waits for them, and re-layouts: 8.98 us -> none
    another operation x5, other arithmetic: 0.02 us -> 8.72 us
  transfers between devices with their start and end apart: 17 -> 17, of which waited for: 11 -> 10; matrix products, arithmetic and copies ran while one was open for 34% -> 12% of each run, Pallas kernels for 0% -> 15%
where the time goes in v4:
time: 604 us; the launch traced here: 596 us
  waiting for transfers between devices  322 us (53%)
  Pallas kernels  89.5 us (15%)
  local copies, waits for them, and re-layouts  78.7 us (13%)
  matrix products  41.8 us (7%)
  other arithmetic  35.5 us (6%)
  between operations  15.3 us (3%)
  blocking collectives  10.3 us (2%)
    psum x1, waiting for transfers between devices, on_device(): lax.psum(lax.psum_scatter(late, 'shard', scatter_dimension=0, tiled=True)...  79.8 us
    reduce_scatter x1, waiting for transfers between devices, on_device(): lax.psum_scatter(dkv_partial, 'ctx', scatter_dimension=0, tiled=True)  66.3 us
    all_gather x3, waiting for transfers between devices, on_device(): kv_chunks.append(lax.all_gather(outgoing, 'ctx', axis=0, tiled=True))  60.3 us
    pallas_call x3, Pallas kernels, attend_back(): pl.pallas_call(functools.partial(_attend_back_kernel, heads=heads, factor...  55.8 us
    all_gather x1, waiting for transfers between devices, on_device(): lax.all_gather(jnp.concatenate([output_weight, inner_weight, outer_weight...  48.9 us
    pallas_call x3, Pallas kernels, attend(): pl.pallas_call(functools.partial(_attend_kernel, heads=heads, factor=fact...  33.7 us
    all_gather x1, waiting for transfers between devices, on_device(): lax.all_gather(jnp.concatenate([key_weight, value_weight, shard_columns,...  31.7 us
    unnamed x10, waiting for transfers between devices  28.9 us
  transfers between devices with their start and end apart: 17, of which 10 were waited for; matrix products, arithmetic and copies ran while one was open for 12% of the time, Pallas kernels for 15%

profile of v4, /device:TPU:0, one launch (start us, length us, event | category | flops | bytes accessed | tf_op | source)
XLA Modules:
  0.0 595.9 jit_solution(16802030058225040958)
XLA Ops:
  16.6 31.7 %all-gather.6.cloned.1.call-done = bf16[768,780]{1,0:T(8,128)(2,1)} async-done(((bf16[192,780]{1,0:T(8,128)(2,1)}), bf16[768,780]{1,0:T(8,128)(2,1)}) %all-gather.6.cloned.1.call-update) | async-done | bytes 1198096 | tf_op jit(solution)/shard_map/all_gather | solution.py:209
  58.3 10.3 %all_gather.18 = bf16[768,384]{1,0:T(8,128)(2,1)S(1)} all-gather(bf16[192,384]{1,0:T(8,128)(2,1)S(1)} %copy-done.22), channel_id=1, replica_groups=mesh['shard'=4,'ctx'=4,'tp'=2] {'shard'}, dimensions={0}, use_global_device_ids=true | all-gather | bytes 737280 | tf_op jit(solution)/shard_map/all_gather | solution.py:213
  70.3 15.7 %all-gather.8.cloned.1.call-done.kv_ref = bf16[2560,256]{1,0:T(8,128)(2,1)} async-done(((bf16[640,256]{1,0:T(8,128)(2,1)}), bf16[2560,256]{1,0:T(8,128)(2,1)}) %all-gather.8.cloned.1.call-update) | async-done | bytes 1310736 | tf_op jit(solution)/shard_map/all_gather | solution.py:247
  86.0 11.2 %shard_map.305 = (bf16[640,128]{1,0:T(8,128)(2,1)}, f32[640,2]{1,0:T(8,128)}) custom-call(s32[1]{0:T(128)S(6)} %copy.95.length_ref, bf16[640,128]{1,0:T(8,128)(2,1)} %get-tuple-element.154.q_ref, bf16[2560,256]{1,0:T(8,128)(2,1)} %all-gather.8.cloned.1.call-done.kv_ref), custom_call_target="tpu_custom_call" | custom-call | flops 838860800 | bytes 1638400 | tf_op jit(solution)/shard_map/pallas_call | solution.py:52
  97.2 22.6 %all-gather.10.cloned.1.call-done.kv_ref = bf16[2560,256]{1,0:T(8,128)(2,1)} async-done(((bf16[640,256]{1,0:T(8,128)(2,1)}), bf16[2560,256]{1,0:T(8,128)(2,1)}) %all-gather.10.cloned.1.call-update) | async-done | bytes 1310736 | tf_op jit(solution)/shard_map/all_gather | solution.py:247
  119.8 11.2 %shard_map.306 = (bf16[640,128]{1,0:T(8,128)(2,1)}, f32[640,2]{1,0:T(8,128)}) custom-call(s32[1]{0:T(128)S(6)} %copy.95.length_ref, bf16[640,128]{1,0:T(8,128)(2,1)} %get-tuple-element.153.q_ref, bf16[2560,256]{1,0:T(8,128)(2,1)} %all-gather.10.cloned.1.call-done.kv_ref), custom_call_target="tpu_custom_call" | custom-call | flops 838860800 | bytes 1638400 | tf_op jit(solution)/shard_map/pallas_call | solution.py:52
  131.0 21.9 %all-gather.12.cloned.1.call-done.kv_ref = bf16[2560,256]{1,0:T(8,128)(2,1)} async-done(((bf16[640,256]{1,0:T(8,128)(2,1)}), bf16[2560,256]{1,0:T(8,128)(2,1)}) %all-gather.12.cloned.1.call-update) | async-done | bytes 1310736 | tf_op jit(solution)/shard_map/all_gather | solution.py:247
  152.9 11.4 %shard_map.307 = (bf16[640,128]{1,0:T(8,128)(2,1)}, f32[640,2]{1,0:T(8,128)}) custom-call(s32[1]{0:T(128)S(6)} %copy.95.length_ref, bf16[640,128]{1,0:T(8,128)(2,1)} %get-tuple-element.152.q_ref, bf16[2560,256]{1,0:T(8,128)(2,1)} %all-gather.12.cloned.1.call-done.kv_ref), custom_call_target="tpu_custom_call" | custom-call | flops 838860800 | bytes 1638400 | tf_op jit(solution)/shard_map/pallas_call | solution.py:52
  167.2 48.9 %all-gather.14.cloned.1.call-done = bf16[768,3456]{1,0:T(8,128)(2,1)} async-done(((bf16[192,3456]{1,0:T(8,128)(2,1)}), bf16[768,3456]{1,0:T(8,128)(2,1)}) %all-gather.14.cloned.1.call-update) | async-done | bytes 5308432 | tf_op jit(solution)/shard_map/all_gather | solution.py:218
  225.3 10.1 %multiply_convert_fusion = (bf16[640,1536]{1,0:T(8,128)(2,1)S(1)}, f32[640,1536]{1,0:T(8,128)S(1)}, f32[640,1536]{1,0:T(8,128)S(1)}) fusion(f32[1536]{0:T(1024)S(1)} %dynamic-slice_convert_fusion, bf16[768,3456]{1,0:T(8,128)(2,1)S(1)} %bitcast.36, f32[640,768]{1,0:T(8,128)S(1)} %get-tuple-element.127, f32[768]{0:T(1024)S(1)} %get-tuple-element.106, ...), kind=kOutput, calls=%fused_computation.5 | convolution fusion | flops 1577287680 | bytes 14180352 | tf_op jit(solution)/shard_map/dot_general | solution.py:258
  237.3 3.8 collective-permute-done.2
  252.3 3.8 convolution_convert_fusion.2
  263.9 4.4 multiply_reduce_fusion
  272.9 9.4 %concatenate.54 = bf16[768,3466]{1,0:T(8,128)(2,1)} concatenate(bf16[768,384]{1,0:T(8,128)(2,1)S(1)} %copy.68, bf16[768,1536]{1,0:T(8,128)(2,1)} %convolution_convert_fusion.2, bf16[768,1536]{1,0:T(8,128)(2,1)} %convolution_convert_fusion.1, bf16[768,1]{1,0:T(8,128)(2,1)S(1)} %stack.117, bf16[768,1]{1,0:T(8,128)(2,1)S(1)} %stack.118, bf16[768,1]{1,0:T(8,128)(2,1)S(1)} %stack.119, ...), dimensions={1} | concatenate | bytes 10647552 | tf_op jit(solution)/shard_map/concatenate | solution.py:288
  286.3 18.7 %shard_map.310 = (bf16[640,128]{1,0:T(8,128)(2,1)}, f32[2560,256]{1,0:T(8,128)}) custom-call(s32[1]{0:T(128)S(6)} %copy.95.length_ref, bf16[640,128]{1,0:T(8,128)(2,1)} %get-tuple-element.152.q_ref, bf16[2560,256]{1,0:T(8,128)(2,1)} %all-gather.12.cloned.1.call-done.kv_ref, bf16[640,128]{1,0:T(8,128)(2,1)} %get-tuple-element.146.do_ref, ...), custom_call_target="tpu_custom_call" | custom-call | flops 2097152000 | bytes 4423680 | tf_op jit(solution)/shard_map/pallas_call | solution.py:113
  308.0 18.5 %shard_map.309 = (bf16[640,128]{1,0:T(8,128)(2,1)}, f32[2560,256]{1,0:T(8,128)}) custom-call(s32[1]{0:T(128)S(6)} %copy.95.length_ref, bf16[640,128]{1,0:T(8,128)(2,1)} %get-tuple-element.153.q_ref, bf16[2560,256]{1,0:T(8,128)(2,1)} %all-gather.10.cloned.1.call-done.kv_ref, bf16[640,128]{1,0:T(8,128)(2,1)} %get-tuple-element.147.do_ref, ...), custom_call_target="tpu_custom_call" | custom-call | flops 2097152000 | bytes 4423680 | tf_op jit(solution)/shard_map/pallas_call | solution.py:113
  330.3 18.5 %shard_map.308 = (bf16[640,128]{1,0:T(8,128)(2,1)}, f32[2560,256]{1,0:T(8,128)}) custom-call(s32[1]{0:T(128)S(6)} %copy.95.length_ref, bf16[640,128]{1,0:T(8,128)(2,1)} %get-tuple-element.154.q_ref, bf16[2560,256]{1,0:T(8,128)(2,1)} %all-gather.8.cloned.1.call-done.kv_ref, bf16[640,128]{1,0:T(8,128)(2,1)} %get-tuple-element.148.do_ref, ...), custom_call_target="tpu_custom_call" | custom-call | flops 2097152000 | bytes 4423680 | tf_op jit(solution)/shard_map/pallas_call | solution.py:113
  359.5 66.3 %reduce-scatter.8.cloned.1.call-done = bf16[640,768]{1,0:T(8,128)(2,1)} async-done(((bf16[2560,768]{1,0:T(8,128)(2,1)}), bf16[640,768]{1,0:T(8,128)(2,1)}) %reduce-scatter.8.cloned.1.call-update) | async-done | bytes 983056 | tf_op jit(solution)/shard_map/reduce_scatter | solution.py:319
  436.1 4.2 fusion.6
  440.4 8.9 %concatenate.59 = bf16[768,1154]{0,1:T(8,128)(2,1)} concatenate(bf16[768,1152]{0,1:T(8,128)(2,1)} %fusion.6, bf16[768,1]{0,1:T(2,128)(2,1)S(1)} %bitcast.38, bf16[768,1]{0,1:T(2,128)(2,1)S(1)} %bitcast.37), dimensions={1} | concatenate | bytes 3545088 | tf_op jit(solution)/shard_map/concatenate | solution.py:347
  449.4 3.9 copy.79
  454.8 4.1 fusion.24
  459.4 28.7 %reduce-scatter.10.cloned.1.call-done = bf16[192,1154]{1,0:T(8,128)(2,1)} async-done(((bf16[768,1154]{1,0:T(8,128)(2,1)}), bf16[192,1154]{1,0:T(8,128)(2,1)}) %reduce-scatter.10.cloned.1.call-update) | async-done | bytes 443152
  494.1 79.8 %all-reduce.3.cloned.1.call-done = (bf16[192,1154]{0,1:T(8,128)(2,1)}, bf16[192,3466]{1,0:T(8,128)(2,1)}) async-done(((bf16[192,1154]{0,1:T(8,128)(2,1)}, bf16[192,3466]{1,0:T(8,128)(2,1)}), (bf16[192,1154]{0,1:T(8,128)(2,1)}, bf16[192,3466]{1,0:T(8,128)(2,1)})) %all-reduce.3.cloned.1.call-update) | async-done | bytes 1774096 | tf_op jit(solution)/shard_map/psum | solution.py:355
  (206 shorter events, 112.2 us)
Async XLA Ops:
  7.2 41.1 %copy-start.9 = (bf16[640,768]{1,0:T(8,128)(2,1)S(1)}, bf16[640,768]{1,0:T(8,128)(2,1)}, u32[]{:S(2)}) copy-start(bf16[640,768]{1,0:T(8,128)(2,1)} %param.18) | copy-start | bytes 2949124
  7.2 41.1 %all-gather.6.cloned.1.call-start = ((), (), s32[]{:S(2)}) async-start(), calls=%async_computation.3 | async-start | bytes 1720320 | tf_op jit(solution)/shard_map/all_gather | solution.py:209
  8.1 5.0 collective-permute-start
  16.5 69.5 %all-gather.8.cloned.1.call-start = ((), (), s32[]{:S(2)}) async-start(), calls=%async_computation.4 | async-start | bytes 1638400 | tf_op jit(solution)/shard_map/all_gather | solution.py:247
  53.3 66.5 %all-gather.10.cloned.1.call-start = ((), (), s32[]{:S(2)}) async-start(), calls=%async_computation.5 | async-start | bytes 1638400 | tf_op jit(solution)/shard_map/all_gather | solution.py:247
  54.2 98.7 %all-gather.12.cloned.1.call-start = ((), (), s32[]{:S(2)}) async-start(), calls=%async_computation.6 | async-start | bytes 1638400 | tf_op jit(solution)/shard_map/all_gather | solution.py:247
  55.0 13.6 %copy-start.19 = (bf16[768,1]{1,0:T(8,128)(2,1)S(1)}, bf16[768,1]{1,0:T(8,128)(2,1)}, u32[]{:S(2)}) copy-start(bf16[768,1]{1,0:T(8,128)(2,1)} %get-tuple-element.132) | copy-start | bytes 4612
  55.0 161.1 %all-gather.14.cloned.1.call-start = ((), (), s32[]{:S(2)}) async-start(), calls=%async_computation.7 | async-start | bytes 6635520 | tf_op jit(solution)/shard_map/all_gather | solution.py:218
  57.6 295.8 %reduce-scatter.6.cloned.1.call-start = ((), (), s32[]{:S(2)}) async-start(), calls=%async_computation.8 | async-start | bytes 6881280 | tf_op jit(solution)/shard_map/reduce_scatter | solution.py:302
  68.6 28.5 %copy-start.17 = (bf16[768,384]{1,0:T(8,128)(2,1)}, bf16[768,384]{1,0:T(8,128)(2,1)S(1)}, u32[]{:S(2)}) copy-start(bf16[768,384]{1,0:T(8,128)(2,1)S(1)} %all_gather.18) | copy-start | bytes 1769476
  152.9 11.4 %copy-start.20 = (bf16[640,128]{1,0:T(8,128)(2,1)S(1)}, bf16[640,128]{1,0:T(8,128)(2,1)}, u32[]{:S(2)}) copy-start(bf16[640,128]{1,0:T(8,128)(2,1)} %get-tuple-element.31) | copy-start | bytes 491524
  152.9 12.1 %copy-start.21 = (bf16[640,128]{1,0:T(8,128)(2,1)S(1)}, bf16[640,128]{1,0:T(8,128)(2,1)}, u32[]{:S(2)}) copy-start(bf16[640,128]{1,0:T(8,128)(2,1)} %get-tuple-element.32) | copy-start | bytes 491524
  218.0 4.2 collective-permute-start.1
  237.1 4.0 collective-permute-start.2
  245.8 10.4 %copy-start.3 = (f32[640,768]{1,0:T(8,128)}, f32[640,768]{1,0:T(8,128)S(1)}, u32[]{:S(2)}) copy-start(f32[640,768]{1,0:T(8,128)S(1)} %get-tuple-element.118) | copy-start | bytes 5898244
  251.8 12.0 %collective-permute-start.3 = (f32[640,768]{1,0:T(8,128)}, f32[640,768]{1,0:T(8,128)}, u32[]{:S(2)}, u32[]{:S(2)}) collective-permute-start(f32[640,768]{1,0:T(8,128)} %fusion.16), channel_id=1, source_target_pairs={{0,1},{1,0},{2,3},{3,2},{4,5},{5,4},{6,7},{7,6},{8,9},{9,8},{10,11... | collective-permute-start | bytes 5898248 | tf_op jit(solution)/shard_map/ppermute | solution.py:153
  252.0 9.5 %collective-permute-start.4 = (bf16[1536]{0:T(1024)(128)(2,1)S(1)}, bf16[1536]{0:T(1024)(128)(2,1)S(1)}, u32[]{:S(2)}, u32[]{:S(2)}) collective-permute-start(bf16[1536]{0:T(1024)(128)(2,1)S(1)} %get-tuple-element.168), channel_id=1, source_target_pairs={{0,1},{1,0},{2,3},{3,2},{4,5},{5,4},{6,7},{7,6},{8,9},{9,8},{10,11... | collective-permute-start | bytes 9224 | tf_op jit(solution)/shard_map/ppermute | solution.py:159
  282.3 143.6 %reduce-scatter.8.cloned.1.call-start = ((), (), s32[]{:S(2)}) async-start(), calls=%async_computation.9 | async-start | bytes 4915200 | tf_op jit(solution)/shard_map/reduce_scatter | solution.py:319
  353.4 134.7 %reduce-scatter.10.cloned.1.call-start = ((), (), s32[]{:S(2)}) async-start(), calls=%async_computation.10 | async-start | bytes 2457600
  355.4 84.9 %collective-permute-start.6 = (bf16[384]{0:T(512)(128)(2,1)S(1)}, bf16[384]{0:T(512)(128)(2,1)S(1)}, u32[]{:S(2)}, u32[]{:S(2)}) collective-permute-start(bf16[384]{0:T(512)(128)(2,1)S(1)} %convert_reduce_fusion.2), channel_id=1, source_target_pairs={{0,1},{1,0},{2,3},{3,2},{4,5},{5,4},{6,7},{7,6},{8,9},{9,8},{10,11... | collective-permute-start | bytes 2312 | tf_op jit(solution)/shard_map/ppermute | solution.py:159
  425.8 10.3 %copy-start.11 = (bf16[640,768]{1,0:T(8,128)(2,1)S(1)}, bf16[640,768]{1,0:T(8,128)(2,1)}, u32[]{:S(2)}) copy-start(bf16[640,768]{1,0:T(8,128)(2,1)} %param.18) | copy-start | bytes 2949124
  432.8 7.5 %collective-permute-start.7 = (bf16[384]{0:T(512)(128)(2,1)S(1)}, bf16[384]{0:T(512)(128)(2,1)S(1)}, u32[]{:S(2)}, u32[]{:S(2)}) collective-permute-start(bf16[384]{0:T(512)(128)(2,1)S(1)} %convert_reduce_fusion.1), channel_id=1, source_target_pairs={{0,1},{1,0},{2,3},{3,2},{4,5},{5,4},{6,7},{7,6},{8,9},{9,8},{10,11... | collective-permute-start | bytes 2312 | tf_op jit(solution)/shard_map/ppermute | solution.py:159
  453.3 120.5 %all-reduce.3.cloned.1.call-start = ((), (), s32[]{:S(2)}) async-start(), calls=%async_computation.11 | async-start | bytes 3940352 | tf_op jit(solution)/shard_map/psum | solution.py:355
  458.9 31.4 %collective-permute-start.5 = (f32[640,768]{1,0:T(8,128)}, f32[640,768]{1,0:T(8,128)}, u32[]{:S(2)}, u32[]{:S(2)}) collective-permute-start(f32[640,768]{1,0:T(8,128)} %fusion.24), channel_id=1, source_target_pairs={{0,1},{1,0},{2,3},{3,2},{4,5},{5,4},{6,7},{7,6},{8,9},{9,8},{10,11... | collective-permute-start | bytes 5898248 | tf_op jit(solution)/shard_map/ppermute | solution.py:153
  (22 other events, 58.1 us)
Sparse Core Ops, SparseCore 0:
  16.6 31.5 all-gather.5
  53.4 32.5 all-gather.7
  88.1 31.6 all-gather.9
  121.2 31.6 all-gather.11
  155.1 60.9 all-gather.13
  282.4 63.4 reduce-scatter.5
  353.5 72.2 reduce-scatter.7
  453.4 34.6 reduce-scatter.9
  491.2 82.5 all-reduce.2
